TPU v7x, 32 devices: a whole 2x2x4 slice. The times are simulated.
32 devices in a mesh: groups: 2 (over y), tensor: 8 (over z, x), dp: 2 (over core).
Axes of the slice: x: 2, y: 2, z: 4, core: 2. Of those that a mesh axis runs over, the one named last changes fastest.
Arguments:
- hidden: bfloat16 [2400, 8192], P(('groups', 'dp'), 'tensor'), parts along dimension 0, may hold values from -6 to 6
- norm_gain: float32 [8192], replicated, may hold values from 0.1 to 1.9
- query_weight: bfloat16 [8192, 8192], P('dp', 'tensor'), may hold values from -0.09375 to 0.09375
- query_keep: int32 [128, 128], P('dp', 'tensor'), may hold values 0 or 1
- kv_weight: bfloat16 [2048, 8192], P('tensor', 'dp'), may hold values from -0.0625 to 0.0625
- out_weight: bfloat16 [8192, 8192], P('tensor', 'dp'), may hold values from -0.5 to 0.5
- out_keep: int32 [128, 128], P('tensor', 'dp'), may hold values 0 or 1
- pair_lengths: int32 [4, 4], P(('groups', 'dp')), parts along dimension 0, may hold values from 1 to 300, 600 in all within a row
- premise_lengths: int32 [4, 4], P(('groups', 'dp')), parts along dimension 0, may hold values from 1 to 299
Outputs:
- attn_out: bfloat16 [2400, 8192], P(('groups', 'dp'), 'tensor'), parts along dimension 0
There are 2 independent parts, one for each index of `groups`. A program takes and returns all parts, laid end to end along the dimension named above; an argument that names none is the same for every part. Nothing has to cross between parts.
Inputs may be any that keep to these rules, and one draw needn't show every extreme that they name: `pair_lengths`: each row lists the 4 pair lengths of one batch in order; they sum to 600.
All inputs are finite; a program needn't handle non-finite values. No bound on the sum of `query_keep` or of `out_keep` on one device may be relied on, other than what follows from the above.
Results may differ from a plain program's by a relative error of at most 0.01.
Values may be sent and summed in bfloat16 or wider, within the bound.
No kernel may reach another device: no remote copies, remote signals or barrier semaphores. Data moves between devices by JAX's collectives and lax.ppermute only.
A program may use at most 192 MiB of HBM per device.

v0:
```python
import jax
import jax.numpy as jnp
import numpy as np
from jax import lax
from jax.sharding import PartitionSpec as P

HEADS = 64
KVH = 8
HD = 128


def rotate_pairs(values, positions):
    half_width = values.shape[-1] // 2
    inverse = 500000.0 ** (-(jnp.arange(half_width, dtype=jnp.float32) * 2.0 / values.shape[-1]))
    angles = positions[:, None] * inverse[None, :]
    cosine = jnp.cos(angles)[:, None, :]
    sine_part = jnp.sin(angles)[:, None, :]
    first_half = values[..., :half_width]
    second_half = values[..., half_width:]
    return jnp.concatenate(
        [
            first_half * cosine - second_half * sine_part,
            second_half * cosine + first_half * sine_part,
        ],
        axis=-1,
    )


def pair_layout(lengths, premise, count):
    pair_ends = jnp.cumsum(lengths)
    pair_starts = pair_ends - lengths
    position = jnp.arange(count, dtype=jnp.int32)
    pair_index = jnp.sum((position[:, None] >= pair_ends[None, :]).astype(jnp.int32), axis=1)
    one_hot = (
        pair_index[:, None] == jnp.arange(lengths.shape[0], dtype=jnp.int32)[None, :]
    ).astype(jnp.int32)
    offset = position - jnp.sum(one_hot * pair_starts[None, :], axis=1)
    premise_used = jnp.minimum(premise, lengths - 1)
    in_premise = offset < jnp.sum(one_hot * premise_used[None, :], axis=1)
    allowed = (pair_index[:, None] == pair_index[None, :]) & (
        in_premise[None, :] | jnp.logical_not(in_premise)[:, None]
    )
    return (offset.astype(jnp.float32), allowed)


def prune(weight, keep):
    blocks = weight.reshape(
        keep.shape[0],
        weight.shape[0] // keep.shape[0],
        keep.shape[1],
        weight.shape[1] // keep.shape[1],
    )
    blocks = blocks * keep.astype(weight.dtype)[:, None, :, None]
    return blocks.reshape(weight.shape)


def ring_order(z_size, x_size):
    if x_size == 1 or z_size == 1:
        return list(range(z_size * x_size))
    cycle = [(z, 0) for z in range(z_size)]
    for step, z in enumerate(range(z_size - 1, -1, -1)):
        xs = list(range(1, x_size))
        cycle += [(z, x) for x in (xs if step % 2 == 0 else xs[::-1])]
    return [z * x_size + x for z, x in cycle]


def fast_prune(weight, keep):
    rows, cols = weight.shape
    step_r, step_c = rows // keep.shape[0], cols // keep.shape[1]
    mask = jnp.repeat(keep.astype(weight.dtype), step_c, axis=1)
    return (weight.reshape(keep.shape[0], step_r, cols) * mask[:, None, :]).reshape(rows, cols)


def make_fast(n, order):
    position_of = np.zeros(n, np.int32)
    for p, t in enumerate(order):
        position_of[t] = p
    order_arr = np.asarray(order, np.int32)
    both = ("tensor", "dp")
    ring_pairs = [(order[i] * 2, order[(i + 1) % n] * 2) for i in range(n)] + [
        (order[i] * 2 + 1, order[(i - 1) % n] * 2 + 1) for i in range(n)
    ]

    def on_device(
        hidden,
        norm_gain,
        query_weight,
        query_keep,
        kv_weight,
        out_weight,
        out_keep,
        pair_lengths,
        premise_lengths,
    ):
        tensor_rank = lax.axis_index("tensor")
        dp_rank = lax.axis_index("dp")
        pos = jnp.asarray(position_of)[tensor_rank]
        ring = jnp.asarray(order_arr)
        sign = 1 - 2 * dp_rank
        total_rows, feat = hidden.shape
        head_local = query_weight.shape[1] // HD

        query_full = fast_prune(
            lax.all_gather(query_weight, "dp", axis=0, tiled=True),
            lax.all_gather(query_keep, "dp", axis=0, tiled=True),
        )
        kv_full = lax.all_gather(kv_weight, "dp", axis=1, tiled=True)
        out_full = fast_prune(
            lax.all_gather(out_weight, "dp", axis=1, tiled=True),
            lax.all_gather(out_keep, "dp", axis=1, tiled=True),
        )

        split = (total_rows // 2 + 7) // 8 * 8
        moving = [hidden[:split], hidden[split:]]
        arrived = [[moving[0]], [moving[1]]]
        sources = [tensor_rank]
        for s in range(n - 1):
            sources.append(ring[(pos - sign * (s + 1)) % n])
            for i in range(2):
                moving[i] = lax.ppermute(moving[i], both, ring_pairs)
                arrived[i].append(moving[i])
        wholes = [jnp.concatenate(arrived[i], axis=1) for i in range(2)]
        norm_gain = jnp.concatenate(
            [lax.dynamic_slice_in_dim(norm_gain, src * feat, feat) for src in sources]
        )
        query_full = jnp.concatenate(
            [lax.dynamic_slice_in_dim(query_full, src * feat, feat, axis=0) for src in sources],
            axis=0,
        )
        kv_full = jnp.concatenate(
            [lax.dynamic_slice_in_dim(kv_full, src * feat, feat, axis=1) for src in sources],
            axis=1,
        )

        offsets, allowed = pair_layout(pair_lengths[0], premise_lengths[0], total_rows)
        low = tensor_rank < n // 2
        even = tensor_rank % 2 == 0
        pairs_a = [(s, 2 * s) if s < n // 2 else (s, 2 * (s - n // 2) + 1) for s in range(n)]
        pairs_b = [(s, 2 * s + 1) if s < n // 2 else (s, 2 * (s - n // 2)) for s in range(n)]
        contract = (((1,), (1,)), ((), ()))
        query_parts, key_parts, value_parts = [], [], []
        for i in range(2):
            rows_float = wholes[i].astype(jnp.float32)
            mean_square = jnp.mean(rows_float * rows_float, axis=-1, keepdims=True)
            normed = (rows_float * lax.rsqrt(mean_square + 1e-05) * norm_gain).astype(jnp.bfloat16)
            query_parts.append(jnp.dot(normed, query_full, preferred_element_type=jnp.float32))
            kv_piece = lax.dot_general(
                normed, kv_full, contract, preferred_element_type=jnp.float32
            ).astype(jnp.bfloat16)
            lo_cols = kv_piece[:, :HD]
            hi_cols = kv_piece[:, HD:]
            got_a = lax.ppermute(jnp.where(low, lo_cols, hi_cols), "tensor", pairs_a)
            got_b = lax.ppermute(jnp.where(low, hi_cols, lo_cols), "tensor", pairs_b)
            key_parts.append(jnp.where(even, got_a, got_b))
            value_parts.append(jnp.where(even, got_b, got_a))
        queries_raw = jnp.concatenate(query_parts, axis=0)
        key_head = jnp.concatenate(key_parts, axis=0)
        value_head = jnp.concatenate(value_parts, axis=0)

        queries = rotate_pairs(queries_raw.reshape(total_rows, head_local, HD), offsets).astype(
            jnp.bfloat16
        )
        keys = rotate_pairs(key_head.astype(jnp.float32)[:, None, :], offsets)[:, 0, :].astype(
            jnp.bfloat16
        )
        scale = HD ** (-0.5)
        starts = [0, split]
        sizes = [split, total_rows - split]

        def context_rows(i, q_rows):
            mask = lax.slice_in_dim(allowed, starts[i], starts[i] + sizes[i], axis=0)
            scores = jnp.einsum("qhd,kd->hqk", q_rows, keys, preferred_element_type=jnp.float32) * scale
            weighted = jnp.where(mask[None, :, :], jnp.exp(scores), 0.0)
            probs = (weighted / jnp.sum(weighted, axis=-1, keepdims=True)).astype(jnp.bfloat16)
            context = jnp.einsum(
                "hqk,kd->qhd", probs, value_head, preferred_element_type=jnp.float32
            ).astype(jnp.bfloat16)
            return context.reshape(sizes[i], head_local * HD)

        def chunk(context, dest_pos):
            cols = lax.dynamic_slice_in_dim(out_full, ring[dest_pos % n] * feat, feat, axis=1)
            return jnp.dot(context, cols, preferred_element_type=jnp.float32)

        parts = []
        for i in range(2):
            q_rows = lax.slice_in_dim(queries, starts[i], starts[i] + sizes[i], axis=0)
            if i > 0:
                q_rows, _ = lax.optimization_barrier((q_rows, parts[0][0]))
            context = context_rows(i, q_rows)
            mine = [chunk(context, pos + sign * (n - 1 - s)) for s in range(n)]
            parts.append([mine[0].astype(jnp.bfloat16)] + lax.optimization_barrier(mine[1:]))
        acc = [None, None]
        for s in range(n - 1):
            for i in range(2):
                if acc[i] is None:
                    send = parts[i][0]
                else:
                    send = (parts[i][s] + acc[i].astype(jnp.float32)).astype(jnp.bfloat16)
                acc[i] = lax.ppermute(send, both, ring_pairs)
        total = jnp.concatenate(
            [parts[i][n - 1] + acc[i].astype(jnp.float32) for i in range(2)], axis=0
        )
        return total.astype(jnp.bfloat16)

    return on_device


def generic(
    hidden,
    norm_gain,
    query_weight,
    query_keep,
    kv_weight,
    out_weight,
    out_keep,
    pair_lengths,
    premise_lengths,
):
    tensor_rank = lax.axis_index("tensor")
    total_rows = hidden.shape[0]
    head_local = query_weight.shape[1] // HD
    query_pruned = prune(query_weight, query_keep)
    out_pruned = prune(out_weight, out_keep)
    query_full = lax.all_gather(query_pruned, "dp", axis=0, tiled=True)
    kv_full, out_full = (
        lax.all_gather(kv_weight, "dp", axis=1, tiled=True),
        lax.all_gather(out_pruned, "dp", axis=1, tiled=True),
    )
    whole = lax.all_gather(hidden, "tensor", axis=1, tiled=True)
    rows_float = whole.astype(jnp.float32)
    mean_square = jnp.mean(rows_float * rows_float, axis=-1, keepdims=True)
    normed = (rows_float * lax.rsqrt(mean_square + 1e-05) * norm_gain).astype(jnp.bfloat16)
    queries_raw = jnp.dot(normed, query_full, preferred_element_type=jnp.float32)
    kv_piece = lax.dot_general(
        normed, kv_full, (((1,), (1,)), ((), ())), preferred_element_type=jnp.float32
    ).astype(jnp.bfloat16)
    kv_whole = lax.all_gather(kv_piece, "tensor", axis=1, tiled=True)
    offsets, allowed = pair_layout(pair_lengths[0], premise_lengths[0], total_rows)
    queries = rotate_pairs(queries_raw.reshape(total_rows, head_local, HD), offsets).astype(
        jnp.bfloat16
    )
    keys_all = rotate_pairs(
        kv_whole[:, : KVH * HD].reshape(total_rows, KVH, HD).astype(jnp.float32), offsets
    ).astype(jnp.bfloat16)
    values_all = kv_whole[:, KVH * HD :].reshape(total_rows, KVH, HD)
    chosen = (tensor_rank * head_local + jnp.arange(head_local, dtype=jnp.int32)) // (HEADS // KVH)
    keys_used = jnp.take(keys_all, chosen, axis=1)
    values_used = jnp.take(values_all, chosen, axis=1)
    scale = HD ** (-0.5)
    scores = (
        jnp.einsum("qhd,khd->hqk", queries, keys_used, preferred_element_type=jnp.float32) * scale
    )
    weighted = jnp.where(allowed[None, :, :], jnp.exp(scores), 0.0)
    probs = (weighted / jnp.sum(weighted, axis=-1, keepdims=True)).astype(jnp.bfloat16)
    context = jnp.einsum(
        "hqk,khd->qhd", probs, values_used, preferred_element_type=jnp.float32
    ).astype(jnp.bfloat16)
    context = context.reshape(total_rows, head_local * HD)
    terms = jnp.dot(context, out_full, preferred_element_type=jnp.float32)
    mixed = lax.psum_scatter(terms, "tensor", scatter_dimension=1, tiled=True)
    return mixed.astype(jnp.bfloat16)


def solution(mesh):
    placed = (
        P(("groups", "dp"), "tensor"),
        P(),
        P("dp", "tensor"),
        P("dp", "tensor"),
        P("tensor", "dp"),
        P("tensor", "dp"),
        P("tensor", "dp"),
        P(("groups", "dp"), None),
        P(("groups", "dp"), None),
    )
    n = mesh.shape["tensor"]
    if n == KVH and mesh.shape["dp"] == 2:
        coords = [getattr(d, "coords", None) for d in mesh.devices.reshape(-1)]
        z_size, x_size = n, 1
        if all(c is not None for c in coords):
            xs = sorted({c[0] for c in coords})
            zs = sorted({c[2] for c in coords})
            if len(xs) * len(zs) == n:
                z_size, x_size = len(zs), len(xs)
        body = make_fast(n, ring_order(z_size, x_size))
    else:
        body = generic
    return jax.shard_map(
        body,
        mesh=mesh,
        in_specs=placed,
        out_specs=P(("groups", "dp"), "tensor"),
        check_vma=False,
    )
```

profile of v0, /device:TPU:0, one launch (start us, length us, event | category | flops | bytes accessed | tf_op | source)
XLA Modules:
  0.0 316.8 jit_solution(3753959648130882574)
XLA Ops:
  10.2 3.1 collective-permute-start.9
  14.2 1.6 collective-permute-start
  30.3 1.6 collective-permute-start.10
  33.4 1.5 collective-permute-start.1
  35.1 5.5 %collective-permute-done.10 = bf16[296,1024]{1,0:T(8,128)(2,1)S(1)} collective-permute-done((bf16[296,1024]{1,0:T(8,128)(2,1)}, bf16[296,1024]{1,0:T(8,128)(2,1)S(1)}, u32[]{:S(2)}, u32[]{:S(2)}) %collective-permute-start.10) | collective-permute-done | bytes 606240 | tf_op jit(solution)/shard_map/ppermute | solution.py:120
  40.6 1.6 collective-permute-start.11
  42.8 4.5 %collective-permute-done.1 = bf16[304,1024]{1,0:T(8,128)(2,1)S(1)} collective-permute-done((bf16[304,1024]{1,0:T(8,128)(2,1)S(1)}, bf16[304,1024]{1,0:T(8,128)(2,1)S(1)}, u32[]{:S(2)}, u32[]{:S(2)}) %collective-permute-start.1) | collective-permute-done | bytes 622624 | tf_op jit(solution)/shard_map/ppermute | solution.py:120
  47.3 1.6 collective-permute-start.2
  49.9 4.0 %collective-permute-done.11 = bf16[296,1024]{1,0:T(8,128)(2,1)} collective-permute-done((bf16[296,1024]{1,0:T(8,128)(2,1)S(1)}, bf16[296,1024]{1,0:T(8,128)(2,1)}, u32[]{:S(2)}, u32[]{:S(2)}) %collective-permute-start.11) | collective-permute-done | bytes 606240 | tf_op jit(solution)/shard_map/ppermute | solution.py:120
  53.9 1.6 collective-permute-start.12
  55.5 5.0 %collective-permute-done.2 = bf16[304,1024]{1,0:T(8,128)(2,1)S(1)} collective-permute-done((bf16[304,1024]{1,0:T(8,128)(2,1)S(1)}, bf16[304,1024]{1,0:T(8,128)(2,1)S(1)}, u32[]{:S(2)}, u32[]{:S(2)}) %collective-permute-start.2) | collective-permute-done | bytes 622624 | tf_op jit(solution)/shard_map/ppermute | solution.py:120
  60.5 1.6 collective-permute-start.3
  67.0 1.8 all-gather
  69.2 1.8 all-gather.1
  72.0 1.1 multiply_cosine_fusion
  73.1 1.5 collective-permute-start.13
  74.6 2.1 constant_dynamic-update-slice_fusion.15
  78.1 2.1 constant_dynamic-update-slice_fusion.14
  81.1 2.1 constant_dynamic-update-slice_fusion.13
  83.4 1.5 collective-permute-start.14
  85.8 4.3 %collective-permute-done.4 = bf16[304,1024]{1,0:T(8,128)(2,1)S(1)} collective-permute-done((bf16[304,1024]{1,0:T(8,128)(2,1)}, bf16[304,1024]{1,0:T(8,128)(2,1)S(1)}, u32[]{:S(2)}, u32[]{:S(2)}) %collective-permute-start.4) | collective-permute-done | bytes 622624 | tf_op jit(solution)/shard_map/ppermute | solution.py:120
  90.1 1.5 collective-permute-start.5
  91.6 2.0 constant_dynamic-update-slice_fusion.12
  93.5 2.0 constant_dynamic-update-slice_fusion.3
  98.2 2.0 constant_dynamic-update-slice_fusion.10
  100.2 3.1 collective-permute-done.5
  103.3 1.5 collective-permute-start.6
  105.6 1.2 dynamic-slice_dynamic-update-slice_fusion.15
  106.9 1.4 dynamic-slice_dynamic-update-slice_fusion.14
  116.0 2.6 fusion.60
  121.3 2.5 fusion.63
  123.8 3.1 collective-permute-start.7
  127.7 2.9 collective-permute-done.7
  131.4 9.7 %bitcast_multiply_fusion.1 = bf16[8192,1024]{1,0:T(8,128)(2,1)S(1)} fusion(bf16[8192,1024]{1,0:T(8,128)(2,1)} %all-gather.8.cloned.1.call-done, bf16[128,1024]{1,0:T(8,128)(2,1)S(1)} %copy.38), kind=kLoop, calls=%fused_computation.1 | loop fusion | flops 8388608 | bytes 33816576 | tf_op jit(solution)/shard_map/mul | solution.py:71
  141.2 1.5 dynamic-slice_dynamic-update-slice_fusion.7
  142.7 1.5 dynamic-slice_dynamic-update-slice_fusion.6
  144.2 1.5 dynamic-slice_dynamic-update-slice_fusion.5
  145.7 1.5 dynamic-slice_dynamic-update-slice_fusion.4
  147.3 1.5 dynamic-slice_dynamic-update-slice_fusion.3
  148.8 1.6 dynamic-slice_dynamic-update-slice_fusion.2
  150.4 1.5 dynamic-slice_dynamic-update-slice_fusion.1
  151.8 1.5 dynamic-slice_dynamic-update-slice_fusion
  153.3 9.4 %fusion.46 = f32[296,1024]{1,0:T(8,128)S(1)} fusion(bf16[8192,1024]{1,0:T(8,128)(2,1)} %dynamic-slice_dynamic-update-slice_fusion, bf16[296,8192]{1,0:T(8,128)(2,1)S(1)} %bitcast.136, f32[8192]{0:T(1024)S(1)} %constant_dynamic-update-slice_fusion.17, f32[296]{0:T(512)S(1)} %add_rsqrt_fusion), kind=kOutput, calls=%fused_computation.66 | convolution fusion | flops 4975755264 | bytes 22873248 | tf_op jit(solution)/shard_map/dot_general | solution.py:146
  162.7 9.0 %fusion.42 = f32[304,1024]{1,0:T(8,128)S(1)} fusion(bf16[8192,1024]{1,0:T(8,128)(2,1)} %dynamic-slice_dynamic-update-slice_fusion, bf16[304,8192]{1,0:T(8,128)(2,1)S(1)} %bitcast.134, f32[8192]{0:T(1024)S(1)} %constant_dynamic-update-slice_fusion.17, f32[304]{0:T(512)S(1)} %add_rsqrt_fusion.1), kind=kOutput, calls=%fused_computation.64 | convolution fusion | flops 5110235136 | bytes 23037120 | tf_op jit(solution)/shard_map/dot_general | solution.py:146
  174.5 2.1 fusion.6
  176.6 10.7 %fusion.58 = bf16[8,38,8,128]{3,2,1,0:T(8,128)(2,1)S(1)} fusion(f32[600,304,8]{0,1,2:T(8,128)S(1)} %get-tuple-element.77, f32[8,304]{1,0:T(8,128)S(1)} %get-tuple-element.76, pred[304,600]{1,0:T(8,128)(4,1)S(1)} %slice.60, bf16[296,128]{0,1:T(8,128)(2,1)S(1)} %get-tuple-element.51, bf16[304,128]{0,1:T(8,128)(2,1)S(1)} %get-tuple-element.49), kind=kOutput, calls=%fused_computation.72 | convolution fusion | flops 380010496 | bytes 6805120 | tf_op jit(solution)/shard_map/hqk,kd->qhd/dot_general | solution.py:175
  187.3 8.2 %bitcast_multiply_fusion = bf16[1024,8192]{1,0:T(8,128)(2,1)S(1)} fusion(bf16[1024,8192]{1,0:T(8,128)(2,1)} %all-gather.10.cloned.1.call-done, bf16[16,8192]{1,0:T(8,128)(2,1)S(1)} %mul.390), kind=kLoop, calls=%fused_computation | loop fusion | flops 8388608 | bytes 33816576 | tf_op jit(solution)/shard_map/mul | solution.py:71
  197.3 5.0 %collective-permute-start.18 = (bf16[304,1024]{1,0:T(8,128)(2,1)S(1)}, bf16[304,1024]{1,0:T(8,128)(2,1)S(1)}, u32[]{:S(2)}, u32[]{:S(2)}) collective-permute-start(bf16[304,1024]{1,0:T(8,128)(2,1)S(1)} %fusion.50), channel_id=1, source_target_pairs={{0,4},{4,8},{8,12},{12,14},{14,10},{10,6},{6,2},{2,0},{1,3},{5,1},... | collective-permute-start | bytes 1867784 | tf_op jit(solution)/shard_map/ppermute | solution.py:199
  202.3 1.9 fusion.7
  204.1 2.2 fusion.59
  218.4 7.5 %collective-permute-done.25 = bf16[296,1024]{1,0:T(8,128)(2,1)S(1)} collective-permute-done((bf16[296,1024]{1,0:T(8,128)(2,1)S(1)}, bf16[296,1024]{1,0:T(8,128)(2,1)S(1)}, u32[]{:S(2)}, u32[]{:S(2)}) %collective-permute-start.25) | collective-permute-done | bytes 606240 | tf_op jit(solution)/shard_map/ppermute | solution.py:199
  227.3 2.5 collective-permute-start.19
  229.8 6.4 %collective-permute-done.26 = bf16[296,1024]{1,0:T(8,128)(2,1)S(1)} collective-permute-done((bf16[296,1024]{1,0:T(8,128)(2,1)S(1)}, bf16[296,1024]{1,0:T(8,128)(2,1)S(1)}, u32[]{:S(2)}, u32[]{:S(2)}) %collective-permute-start.26) | collective-permute-done | bytes 606240 | tf_op jit(solution)/shard_map/ppermute | solution.py:199
  237.4 5.6 %collective-permute-done.19 = bf16[304,1024]{1,0:T(8,128)(2,1)S(1)} collective-permute-done((bf16[304,1024]{1,0:T(8,128)(2,1)S(1)}, bf16[304,1024]{1,0:T(8,128)(2,1)S(1)}, u32[]{:S(2)}, u32[]{:S(2)}) %collective-permute-start.19) | collective-permute-done | bytes 622624 | tf_op jit(solution)/shard_map/ppermute | solution.py:199
  244.1 5.4 %collective-permute-done.27 = bf16[296,1024]{1,0:T(8,128)(2,1)S(1)} collective-permute-done((bf16[296,1024]{1,0:T(8,128)(2,1)S(1)}, bf16[296,1024]{1,0:T(8,128)(2,1)S(1)}, u32[]{:S(2)}, u32[]{:S(2)}) %collective-permute-start.27) | collective-permute-done | bytes 606240 | tf_op jit(solution)/shard_map/ppermute | solution.py:199
  250.5 5.6 %collective-permute-done.20 = bf16[304,1024]{1,0:T(8,128)(2,1)S(1)} collective-permute-done((bf16[304,1024]{1,0:T(8,128)(2,1)S(1)}, bf16[304,1024]{1,0:T(8,128)(2,1)S(1)}, u32[]{:S(2)}, u32[]{:S(2)}) %collective-permute-start.20) | collective-permute-done | bytes 622624 | tf_op jit(solution)/shard_map/ppermute | solution.py:199
  257.2 5.3 %collective-permute-done.28 = bf16[296,1024]{1,0:T(8,128)(2,1)S(1)} collective-permute-done((bf16[296,1024]{1,0:T(8,128)(2,1)S(1)}, bf16[296,1024]{1,0:T(8,128)(2,1)S(1)}, u32[]{:S(2)}, u32[]{:S(2)}) %collective-permute-start.28) | collective-permute-done | bytes 606240 | tf_op jit(solution)/shard_map/ppermute | solution.py:199
  263.7 5.5 %collective-permute-done.21 = bf16[304,1024]{1,0:T(8,128)(2,1)S(1)} collective-permute-done((bf16[304,1024]{1,0:T(8,128)(2,1)S(1)}, bf16[304,1024]{1,0:T(8,128)(2,1)S(1)}, u32[]{:S(2)}, u32[]{:S(2)}) %collective-permute-start.21) | collective-permute-done | bytes 622624 | tf_op jit(solution)/shard_map/ppermute | solution.py:199
  270.4 5.3 %collective-permute-done.29 = bf16[296,1024]{1,0:T(8,128)(2,1)S(1)} collective-permute-done((bf16[296,1024]{1,0:T(8,128)(2,1)S(1)}, bf16[296,1024]{1,0:T(8,128)(2,1)S(1)}, u32[]{:S(2)}, u32[]{:S(2)}) %collective-permute-start.29) | collective-permute-done | bytes 606240 | tf_op jit(solution)/shard_map/ppermute | solution.py:199
  276.9 5.5 %collective-permute-done.22 = bf16[304,1024]{1,0:T(8,128)(2,1)S(1)} collective-permute-done((bf16[304,1024]{1,0:T(8,128)(2,1)S(1)}, bf16[304,1024]{1,0:T(8,128)(2,1)S(1)}, u32[]{:S(2)}, u32[]{:S(2)}) %collective-permute-start.22) | collective-permute-done | bytes 622624 | tf_op jit(solution)/shard_map/ppermute | solution.py:199
  283.6 5.3 %collective-permute-done.30 = bf16[296,1024]{1,0:T(8,128)(2,1)S(1)} collective-permute-done((bf16[296,1024]{1,0:T(8,128)(2,1)S(1)}, bf16[296,1024]{1,0:T(8,128)(2,1)S(1)}, u32[]{:S(2)}, u32[]{:S(2)}) %collective-permute-start.30) | collective-permute-done | bytes 606240 | tf_op jit(solution)/shard_map/ppermute | solution.py:199
  290.0 5.5 %collective-permute-done.23 = bf16[304,1024]{1,0:T(8,128)(2,1)S(1)} collective-permute-done((bf16[304,1024]{1,0:T(8,128)(2,1)S(1)}, bf16[304,1024]{1,0:T(8,128)(2,1)S(1)}, u32[]{:S(2)}, u32[]{:S(2)}) %collective-permute-start.23) | collective-permute-done | bytes 622624 | tf_op jit(solution)/shard_map/ppermute | solution.py:199
  296.7 5.3 %collective-permute-done.31 = bf16[296,1024]{1,0:T(8,128)(2,1)S(1)} collective-permute-done((bf16[296,1024]{1,0:T(8,128)(2,1)S(1)}, bf16[296,1024]{1,0:T(8,128)(2,1)S(1)}, u32[]{:S(2)}, u32[]{:S(2)}) %collective-permute-start.31) | collective-permute-done | bytes 606240 | tf_op jit(solution)/shard_map/ppermute | solution.py:199
  302.3 6.5 %collective-permute-done.24 = bf16[304,1024]{1,0:T(8,128)(2,1)S(1)} collective-permute-done((bf16[304,1024]{1,0:T(8,128)(2,1)S(1)}, bf16[304,1024]{1,0:T(8,128)(2,1)S(1)}, u32[]{:S(2)}, u32[]{:S(2)}) %collective-permute-start.24) | collective-permute-done | bytes 622624 | tf_op jit(solution)/shard_map/ppermute | solution.py:199
  (173 shorter events, 57.2 us)
Async XLA Ops:
  6.5 99.1 %all-gather.6.cloned.1.call-start = ((), (), s32[]{:S(2)}) async-start(), calls=%async_computation | async-start | bytes 6291456 | tf_op jit(solution)/shard_map/all_gather | solution.py:107
  7.3 124.2 %all-gather.8.cloned.1.call-start = ((), (), s32[]{:S(2)}) async-start(), calls=%async_computation.1 | async-start | bytes 25165824 | tf_op jit(solution)/shard_map/all_gather | solution.py:104
  8.0 1.3 copy-start.3
  8.0 7.8 %copy-start.11 = (s32[8]{0:T(128)S(1)}, s32[8]{0:T(128)}, u32[]{:S(2)}) copy-start(s32[8]{0:T(128)} %constant.166.clone) | copy-start | bytes 100
  8.0 19.7 %copy-start.5 = (s32[8]{0:T(128)S(1)}, s32[8]{0:T(128)}, u32[]{:S(2)}) copy-start(s32[8]{0:T(128)} %constant.167.clone) | copy-start | bytes 100
  8.0 179.3 %all-gather.10.cloned.1.call-start = ((), (), s32[]{:S(2)}) async-start(), calls=%async_computation.2 | async-start | bytes 25165824 | tf_op jit(solution)/shard_map/all_gather | solution.py:109
  9.3 20.9 %copy-start.6 = (f32[8192]{0:T(1024)S(1)}, f32[8192]{0:T(1024)}, u32[]{:S(2)}) copy-start(f32[8192]{0:T(1024)} %param.12) | copy-start | bytes 98308
  9.3 23.9 %copy-start.9 = (s32[1,4]{1,0:T(1,128)S(1)}, s32[1,4]{1,0:T(1,128)}, u32[]{:S(2)}) copy-start(s32[1,4]{1,0:T(1,128)} %param.18) | copy-start | bytes 52
  9.3 25.7 %copy-start.10 = (s32[1,4]{1,0:T(1,128)S(1)}, s32[1,4]{1,0:T(1,128)}, u32[]{:S(2)}) copy-start(s32[1,4]{1,0:T(1,128)} %param.19) | copy-start | bytes 52
  9.3 57.7 %copy-start.7 = (s32[64,16]{0,1:T(8,128)S(1)}, s32[64,16]{0,1:T(8,128)}, u32[]{:S(2)}) copy-start(s32[64,16]{0,1:T(8,128)} %param.14) | copy-start | bytes 12292
  9.3 59.9 %copy-start.8 = (s32[16,64]{1,0:T(8,128)S(1)}, s32[16,64]{1,0:T(8,128)}, u32[]{:S(2)}) copy-start(s32[16,64]{1,0:T(8,128)} %param.17) | copy-start | bytes 12292
  10.2 20.1 %collective-permute-start.9 = (bf16[296,1024]{1,0:T(8,128)(2,1)S(1)}, bf16[296,1024]{1,0:T(8,128)(2,1)}, u32[]{:S(2)}, u32[]{:S(2)}) collective-permute-start(bf16[296,1024]{1,0:T(8,128)(2,1)S(1)} %get-tuple-element.45), channel_id=1, source_target_pairs={{0,4},{4,8},{8,12},{12,14},{14,10},{10,6},{6,2},{2,0},{1,3},{5,1},... | collective-permute-start | bytes 1818632 | tf_op jit(solution)/shard_map/ppermute | solution.py:120
  14.2 19.2 %collective-permute-start = (bf16[304,1024]{1,0:T(8,128)(2,1)S(1)}, bf16[304,1024]{1,0:T(8,128)(2,1)S(1)}, u32[]{:S(2)}, u32[]{:S(2)}) collective-permute-start(bf16[304,1024]{1,0:T(8,128)(2,1)S(1)} %get-tuple-element.43), channel_id=1, source_target_pairs={{0,4},{4,8},{8,12},{12,14},{14,10},{10,6},{6,2},{2,0},{1,3},{5,1},... | collective-permute-start | bytes 1867784 | tf_op jit(solution)/shard_map/ppermute | solution.py:120
  30.3 10.3 %collective-permute-start.10 = (bf16[296,1024]{1,0:T(8,128)(2,1)}, bf16[296,1024]{1,0:T(8,128)(2,1)S(1)}, u32[]{:S(2)}, u32[]{:S(2)}) collective-permute-start(bf16[296,1024]{1,0:T(8,128)(2,1)} %collective-permute-done.9), channel_id=1, source_target_pairs={{0,4},{4,8},{8,12},{12,14},{14,10},{10,6},{6,2},{2,0},{1,3},{5,1},... | collective-permute-start | bytes 1818632 | tf_op jit(solution)/shard_map/ppermute | solution.py:120
  33.4 13.9 %collective-permute-start.1 = (bf16[304,1024]{1,0:T(8,128)(2,1)S(1)}, bf16[304,1024]{1,0:T(8,128)(2,1)S(1)}, u32[]{:S(2)}, u32[]{:S(2)}) collective-permute-start(bf16[304,1024]{1,0:T(8,128)(2,1)S(1)} %collective-permute-done), channel_id=1, source_target_pairs={{0,4},{4,8},{8,12},{12,14},{14,10},{10,6},{6,2},{2,0},{1,3},{5,1},... | collective-permute-start | bytes 1867784 | tf_op jit(solution)/shard_map/ppermute | solution.py:120
  40.6 28.4 %copy-start.4 = (bf16[296,1024]{1,0:T(8,128)(2,1)}, bf16[296,1024]{1,0:T(8,128)(2,1)S(1)}, u32[]{:S(2)}) copy-start(bf16[296,1024]{1,0:T(8,128)(2,1)S(1)} %collective-permute-done.10) | copy-start | bytes 1818628
  40.6 13.3 %collective-permute-start.11 = (bf16[296,1024]{1,0:T(8,128)(2,1)S(1)}, bf16[296,1024]{1,0:T(8,128)(2,1)}, u32[]{:S(2)}, u32[]{:S(2)}) collective-permute-start(bf16[296,1024]{1,0:T(8,128)(2,1)S(1)} %collective-permute-done.10), channel_id=1, source_target_pairs={{0,4},{4,8},{8,12},{12,14},{14,10},{10,6},{6,2},{2,0},{1,3},{5,1},... | collective-permute-start | bytes 1818632 | tf_op jit(solution)/shard_map/ppermute | solution.py:120
  47.3 13.2 %collective-permute-start.2 = (bf16[304,1024]{1,0:T(8,128)(2,1)S(1)}, bf16[304,1024]{1,0:T(8,128)(2,1)S(1)}, u32[]{:S(2)}, u32[]{:S(2)}) collective-permute-start(bf16[304,1024]{1,0:T(8,128)(2,1)S(1)} %collective-permute-done.1), channel_id=1, source_target_pairs={{0,4},{4,8},{8,12},{12,14},{14,10},{10,6},{6,2},{2,0},{1,3},{5,1},... | collective-permute-start | bytes 1867784 | tf_op jit(solution)/shard_map/ppermute | solution.py:120
  53.9 19.2 %collective-permute-start.12 = (bf16[296,1024]{1,0:T(8,128)(2,1)}, bf16[296,1024]{1,0:T(8,128)(2,1)}, u32[]{:S(2)}, u32[]{:S(2)}) collective-permute-start(bf16[296,1024]{1,0:T(8,128)(2,1)} %collective-permute-done.11), channel_id=1, source_target_pairs={{0,4},{4,8},{8,12},{12,14},{14,10},{10,6},{6,2},{2,0},{1,3},{5,1},... | collective-permute-start | bytes 1818632 | tf_op jit(solution)/shard_map/ppermute | solution.py:120
  60.5 16.2 %collective-permute-start.3 = (bf16[304,1024]{1,0:T(8,128)(2,1)S(1)}, bf16[304,1024]{1,0:T(8,128)(2,1)}, u32[]{:S(2)}, u32[]{:S(2)}) collective-permute-start(bf16[304,1024]{1,0:T(8,128)(2,1)S(1)} %collective-permute-done.2), channel_id=1, source_target_pairs={{0,4},{4,8},{8,12},{12,14},{14,10},{10,6},{6,2},{2,0},{1,3},{5,1},... | collective-permute-start | bytes 1867784 | tf_op jit(solution)/shard_map/ppermute | solution.py:120
  73.1 10.3 %collective-permute-start.13 = (bf16[296,1024]{1,0:T(8,128)(2,1)}, bf16[296,1024]{1,0:T(8,128)(2,1)S(1)}, u32[]{:S(2)}, u32[]{:S(2)}) collective-permute-start(bf16[296,1024]{1,0:T(8,128)(2,1)} %collective-permute-done.12), channel_id=1, source_target_pairs={{0,4},{4,8},{8,12},{12,14},{14,10},{10,6},{6,2},{2,0},{1,3},{5,1},... | collective-permute-start | bytes 1818632 | tf_op jit(solution)/shard_map/ppermute | solution.py:120
  76.7 13.4 %collective-permute-start.4 = (bf16[304,1024]{1,0:T(8,128)(2,1)}, bf16[304,1024]{1,0:T(8,128)(2,1)S(1)}, u32[]{:S(2)}, u32[]{:S(2)}) collective-permute-start(bf16[304,1024]{1,0:T(8,128)(2,1)} %collective-permute-done.3), channel_id=1, source_target_pairs={{0,4},{4,8},{8,12},{12,14},{14,10},{10,6},{6,2},{2,0},{1,3},{5,1},... | collective-permute-start | bytes 1867784 | tf_op jit(solution)/shard_map/ppermute | solution.py:120
  83.4 14.0 %collective-permute-start.14 = (bf16[296,1024]{1,0:T(8,128)(2,1)S(1)}, bf16[296,1024]{1,0:T(8,128)(2,1)}, u32[]{:S(2)}, u32[]{:S(2)}) collective-permute-start(bf16[296,1024]{1,0:T(8,128)(2,1)S(1)} %collective-permute-done.13), channel_id=1, source_target_pairs={{0,4},{4,8},{8,12},{12,14},{14,10},{10,6},{6,2},{2,0},{1,3},{5,1},... | collective-permute-start | bytes 1818632 | tf_op jit(solution)/shard_map/ppermute | solution.py:120
  90.1 13.2 %collective-permute-start.5 = (bf16[304,1024]{1,0:T(8,128)(2,1)S(1)}, bf16[304,1024]{1,0:T(8,128)(2,1)S(1)}, u32[]{:S(2)}, u32[]{:S(2)}) collective-permute-start(bf16[304,1024]{1,0:T(8,128)(2,1)S(1)} %collective-permute-done.4), channel_id=1, source_target_pairs={{0,4},{4,8},{8,12},{12,14},{14,10},{10,6},{6,2},{2,0},{1,3},{5,1},... | collective-permute-start | bytes 1867784 | tf_op jit(solution)/shard_map/ppermute | solution.py:120
  97.4 17.4 %collective-permute-start.15 = (bf16[296,1024]{1,0:T(8,128)(2,1)}, bf16[296,1024]{1,0:T(8,128)(2,1)S(1)}, u32[]{:S(2)}, u32[]{:S(2)}) collective-permute-start(bf16[296,1024]{1,0:T(8,128)(2,1)} %collective-permute-done.14), channel_id=1, source_target_pairs={{0,4},{4,8},{8,12},{12,14},{14,10},{10,6},{6,2},{2,0},{1,3},{5,1},... | collective-permute-start | bytes 1818632 | tf_op jit(solution)/shard_map/ppermute | solution.py:120
  103.3 16.9 %collective-permute-start.6 = (bf16[304,1024]{1,0:T(8,128)(2,1)S(1)}, bf16[304,1024]{1,0:T(8,128)(2,1)S(1)}, u32[]{:S(2)}, u32[]{:S(2)}) collective-permute-start(bf16[304,1024]{1,0:T(8,128)(2,1)S(1)} %collective-permute-done.5), channel_id=1, source_target_pairs={{0,4},{4,8},{8,12},{12,14},{14,10},{10,6},{6,2},{2,0},{1,3},{5,1},... | collective-permute-start | bytes 1867784 | tf_op jit(solution)/shard_map/ppermute | solution.py:120
  105.6 9.2 %copy-start.1 = (bf16[296,8192]{1,0:T(8,128)(2,1)S(1)}, bf16[296,8192]{1,0:T(8,128)(2,1)}, u32[]{:S(2)}) copy-start(bf16[296,8192]{1,0:T(8,128)(2,1)} %constant_dynamic-update-slice_fusion.10) | copy-start | bytes 14548996
  114.9 3.7 %copy-start.2 = (bf16[296,8192]{1,0:T(8,128)(2,1)}, bf16[296,8192]{1,0:T(8,128)(2,1)S(1)}, u32[]{:S(2)}) copy-start(bf16[296,8192]{1,0:T(8,128)(2,1)S(1)} %constant_dynamic-update-slice_fusion.9) | copy-start | bytes 14548996
  114.9 5.3 %slice-start = ((s8[4980736]{0:T(1024)(128)(4,1)}), s8[4194304]{0:T(1024)(128)(4,1)S(1)}, s32[]{:S(2)}) async-start(s8[4980736]{0:T(1024)(128)(4,1)} %bitcast.131), calls=%async_computation.3 | async-start | bytes 8388608
  116.0 4.2 %slice-start.1 = ((s8[4980736]{0:T(1024)(128)(4,1)}), s8[786432]{0:T(1024)(128)(4,1)S(1)}, s32[]{:S(2)}) async-start(s8[4980736]{0:T(1024)(128)(4,1)} %bitcast.131), calls=%async_computation.4 | async-start | bytes 1572864
  118.6 9.0 %collective-permute-start.16 = (bf16[296,128]{0,1:T(8,128)(2,1)S(1)}, bf16[296,128]{0,1:T(8,128)(2,1)S(1)}, u32[]{:S(2)}, u32[]{:S(2)}) collective-permute-start(bf16[296,128]{0,1:T(8,128)(2,1)S(1)} %get-tuple-element.55), channel_id=1, source_target_pairs={{0,2},{2,6},{4,10},{6,14},{8,0},{10,4},{12,8},{14,12},{1,3},{3,7},... | collective-permute-start | bytes 227336 | tf_op jit(solution)/shard_map/ppermute | solution.py:153
  119.2 8.4 %collective-permute-start.17 = (bf16[296,128]{0,1:T(8,128)(2,1)S(1)}, bf16[296,128]{0,1:T(8,128)(2,1)S(1)}, u32[]{:S(2)}, u32[]{:S(2)}) collective-permute-start(bf16[296,128]{0,1:T(8,128)(2,1)S(1)} %get-tuple-element.56), channel_id=1, source_target_pairs={{0,0},{2,4},{4,8},{6,12},{8,2},{10,6},{12,10},{14,14},{1,1},{3,5},... | collective-permute-start | bytes 227336 | tf_op jit(solution)/shard_map/ppermute | solution.py:152
  120.2 3.6 %copy-start = (bf16[304,8192]{1,0:T(8,128)(2,1)}, bf16[304,8192]{1,0:T(8,128)(2,1)S(1)}, u32[]{:S(2)}) copy-start(bf16[304,8192]{1,0:T(8,128)(2,1)S(1)} %constant_dynamic-update-slice_fusion) | copy-start | bytes 14942212
  123.8 6.7 %collective-permute-start.7 = (bf16[304,128]{0,1:T(8,128)(2,1)S(1)}, bf16[304,128]{0,1:T(8,128)(2,1)S(1)}, u32[]{:S(2)}, u32[]{:S(2)}) collective-permute-start(bf16[304,128]{0,1:T(8,128)(2,1)S(1)} %get-tuple-element.53), channel_id=1, source_target_pairs={{0,2},{2,6},{4,10},{6,14},{8,0},{10,4},{12,8},{14,12},{1,3},{3,7},... | collective-permute-start | bytes 233480 | tf_op jit(solution)/shard_map/ppermute | solution.py:153
  126.9 3.6 %collective-permute-start.8 = (bf16[304,128]{0,1:T(8,128)(2,1)S(1)}, bf16[304,128]{0,1:T(8,128)(2,1)S(1)}, u32[]{:S(2)}, u32[]{:S(2)}) collective-permute-start(bf16[304,128]{0,1:T(8,128)(2,1)S(1)} %get-tuple-element.54), channel_id=1, source_target_pairs={{0,0},{2,4},{4,8},{6,12},{8,2},{10,6},{12,10},{14,14},{1,1},{3,5},... | collective-permute-start | bytes 233480 | tf_op jit(solution)/shard_map/ppermute | solution.py:152
  148.8 4.5 %slice-start.4 = ((s8[4849664]{0:T(1024)(128)(4,1)}), s8[4194304]{0:T(1024)(128)(4,1)S(1)}, s32[]{:S(2)}) async-start(s8[4849664]{0:T(1024)(128)(4,1)} %bitcast.135), calls=%async_computation.7 | async-start | bytes 8388608
  150.4 2.9 slice-start.5
  151.8 10.9 %slice-start.2 = ((s8[4980736]{0:T(1024)(128)(4,1)}), s8[4194304]{0:T(1024)(128)(4,1)S(1)}, s32[]{:S(2)}) async-start(s8[4980736]{0:T(1024)(128)(4,1)} %bitcast.133), calls=%async_computation.5 | async-start | bytes 8388608
  153.3 9.4 %slice-start.3 = ((s8[4980736]{0:T(1024)(128)(4,1)}), s8[786432]{0:T(1024)(128)(4,1)S(1)}, s32[]{:S(2)}) async-start(s8[4980736]{0:T(1024)(128)(4,1)} %bitcast.133), calls=%async_computation.6 | async-start | bytes 1572864
  187.3 9.1 %copy-start.12 = (bf16[8,38,8,128]{3,2,1,0:T(8,128)(2,1)}, bf16[8,38,8,128]{3,2,1,0:T(8,128)(2,1)S(1)}, u32[]{:S(2)}) copy-start(bf16[8,38,8,128]{3,2,1,0:T(8,128)(2,1)S(1)} %fusion.58) | copy-start | bytes 1867780
  197.3 29.8 %collective-permute-start.18 = (bf16[304,1024]{1,0:T(8,128)(2,1)S(1)}, bf16[304,1024]{1,0:T(8,128)(2,1)S(1)}, u32[]{:S(2)}, u32[]{:S(2)}) collective-permute-start(bf16[304,1024]{1,0:T(8,128)(2,1)S(1)} %fusion.50), channel_id=1, source_target_pairs={{0,4},{4,8},{8,12},{12,14},{14,10},{10,6},{6,2},{2,0},{1,3},{5,1},... | collective-permute-start | bytes 1867784 | tf_op jit(solution)/shard_map/ppermute | solution.py:199
  206.3 1.7 copy-start.13
  215.6 10.3 %collective-permute-start.25 = (bf16[296,1024]{1,0:T(8,128)(2,1)S(1)}, bf16[296,1024]{1,0:T(8,128)(2,1)S(1)}, u32[]{:S(2)}, u32[]{:S(2)}) collective-permute-start(bf16[296,1024]{1,0:T(8,128)(2,1)S(1)} %fusion.54), channel_id=1, source_target_pairs={{0,4},{4,8},{8,12},{12,14},{14,10},{10,6},{6,2},{2,0},{1,3},{5,1},... | collective-permute-start | bytes 1818632 | tf_op jit(solution)/shard_map/ppermute | solution.py:199
  226.1 10.1 %collective-permute-start.26 = (bf16[296,1024]{1,0:T(8,128)(2,1)S(1)}, bf16[296,1024]{1,0:T(8,128)(2,1)S(1)}, u32[]{:S(2)}, u32[]{:S(2)}) collective-permute-start(bf16[296,1024]{1,0:T(8,128)(2,1)S(1)} %add_convert_fusion.14), channel_id=1, source_target_pairs={{0,4},{4,8},{8,12},{12,14},{14,10},{10,6},{6,2},{2,0},{1,3},{5,1},... | collective-permute-start | bytes 1818632 | tf_op jit(solution)/shard_map/ppermute | solution.py:199
  227.3 15.6 %collective-permute-start.19 = (bf16[304,1024]{1,0:T(8,128)(2,1)S(1)}, bf16[304,1024]{1,0:T(8,128)(2,1)S(1)}, u32[]{:S(2)}, u32[]{:S(2)}) collective-permute-start(bf16[304,1024]{1,0:T(8,128)(2,1)S(1)} %add_convert_fusion.7), channel_id=1, source_target_pairs={{0,4},{4,8},{8,12},{12,14},{14,10},{10,6},{6,2},{2,0},{1,3},{5,1},... | collective-permute-start | bytes 1867784 | tf_op jit(solution)/shard_map/ppermute | solution.py:199
  236.4 13.0 %collective-permute-start.27 = (bf16[296,1024]{1,0:T(8,128)(2,1)S(1)}, bf16[296,1024]{1,0:T(8,128)(2,1)S(1)}, u32[]{:S(2)}, u32[]{:S(2)}) collective-permute-start(bf16[296,1024]{1,0:T(8,128)(2,1)S(1)} %add_convert_fusion.13), channel_id=1, source_target_pairs={{0,4},{4,8},{8,12},{12,14},{14,10},{10,6},{6,2},{2,0},{1,3},{5,1},... | collective-permute-start | bytes 1818632 | tf_op jit(solution)/shard_map/ppermute | solution.py:199
  243.1 13.0 %collective-permute-start.20 = (bf16[304,1024]{1,0:T(8,128)(2,1)S(1)}, bf16[304,1024]{1,0:T(8,128)(2,1)S(1)}, u32[]{:S(2)}, u32[]{:S(2)}) collective-permute-start(bf16[304,1024]{1,0:T(8,128)(2,1)S(1)} %add_convert_fusion.6), channel_id=1, source_target_pairs={{0,4},{4,8},{8,12},{12,14},{14,10},{10,6},{6,2},{2,0},{1,3},{5,1},... | collective-permute-start | bytes 1867784 | tf_op jit(solution)/shard_map/ppermute | solution.py:199
  249.6 13.0 %collective-permute-start.28 = (bf16[296,1024]{1,0:T(8,128)(2,1)S(1)}, bf16[296,1024]{1,0:T(8,128)(2,1)S(1)}, u32[]{:S(2)}, u32[]{:S(2)}) collective-permute-start(bf16[296,1024]{1,0:T(8,128)(2,1)S(1)} %add_convert_fusion.12), channel_id=1, source_target_pairs={{0,4},{4,8},{8,12},{12,14},{14,10},{10,6},{6,2},{2,0},{1,3},{5,1},... | collective-permute-start | bytes 1818632 | tf_op jit(solution)/shard_map/ppermute | solution.py:199
  256.3 12.9 %collective-permute-start.21 = (bf16[304,1024]{1,0:T(8,128)(2,1)S(1)}, bf16[304,1024]{1,0:T(8,128)(2,1)S(1)}, u32[]{:S(2)}, u32[]{:S(2)}) collective-permute-start(bf16[304,1024]{1,0:T(8,128)(2,1)S(1)} %add_convert_fusion.5), channel_id=1, source_target_pairs={{0,4},{4,8},{8,12},{12,14},{14,10},{10,6},{6,2},{2,0},{1,3},{5,1},... | collective-permute-start | bytes 1867784 | tf_op jit(solution)/shard_map/ppermute | solution.py:199
  262.8 13.0 %collective-permute-start.29 = (bf16[296,1024]{1,0:T(8,128)(2,1)S(1)}, bf16[296,1024]{1,0:T(8,128)(2,1)S(1)}, u32[]{:S(2)}, u32[]{:S(2)}) collective-permute-start(bf16[296,1024]{1,0:T(8,128)(2,1)S(1)} %add_convert_fusion.11), channel_id=1, source_target_pairs={{0,4},{4,8},{8,12},{12,14},{14,10},{10,6},{6,2},{2,0},{1,3},{5,1},... | collective-permute-start | bytes 1818632 | tf_op jit(solution)/shard_map/ppermute | solution.py:199
  269.5 12.9 %collective-permute-start.22 = (bf16[304,1024]{1,0:T(8,128)(2,1)S(1)}, bf16[304,1024]{1,0:T(8,128)(2,1)S(1)}, u32[]{:S(2)}, u32[]{:S(2)}) collective-permute-start(bf16[304,1024]{1,0:T(8,128)(2,1)S(1)} %add_convert_fusion.4), channel_id=1, source_target_pairs={{0,4},{4,8},{8,12},{12,14},{14,10},{10,6},{6,2},{2,0},{1,3},{5,1},... | collective-permute-start | bytes 1867784 | tf_op jit(solution)/shard_map/ppermute | solution.py:199
  275.9 13.0 %collective-permute-start.30 = (bf16[296,1024]{1,0:T(8,128)(2,1)S(1)}, bf16[296,1024]{1,0:T(8,128)(2,1)S(1)}, u32[]{:S(2)}, u32[]{:S(2)}) collective-permute-start(bf16[296,1024]{1,0:T(8,128)(2,1)S(1)} %add_convert_fusion.10), channel_id=1, source_target_pairs={{0,4},{4,8},{8,12},{12,14},{14,10},{10,6},{6,2},{2,0},{1,3},{5,1},... | collective-permute-start | bytes 1818632 | tf_op jit(solution)/shard_map/ppermute | solution.py:199
  282.6 12.9 %collective-permute-start.23 = (bf16[304,1024]{1,0:T(8,128)(2,1)S(1)}, bf16[304,1024]{1,0:T(8,128)(2,1)S(1)}, u32[]{:S(2)}, u32[]{:S(2)}) collective-permute-start(bf16[304,1024]{1,0:T(8,128)(2,1)S(1)} %add_convert_fusion.3), channel_id=1, source_target_pairs={{0,4},{4,8},{8,12},{12,14},{14,10},{10,6},{6,2},{2,0},{1,3},{5,1},... | collective-permute-start | bytes 1867784 | tf_op jit(solution)/shard_map/ppermute | solution.py:199
  289.1 13.0 %collective-permute-start.31 = (bf16[296,1024]{1,0:T(8,128)(2,1)S(1)}, bf16[296,1024]{1,0:T(8,128)(2,1)S(1)}, u32[]{:S(2)}, u32[]{:S(2)}) collective-permute-start(bf16[296,1024]{1,0:T(8,128)(2,1)S(1)} %add_convert_fusion.9), channel_id=1, source_target_pairs={{0,4},{4,8},{8,12},{12,14},{14,10},{10,6},{6,2},{2,0},{1,3},{5,1},... | collective-permute-start | bytes 1818632 | tf_op jit(solution)/shard_map/ppermute | solution.py:199
  295.8 12.9 %collective-permute-start.24 = (bf16[304,1024]{1,0:T(8,128)(2,1)S(1)}, bf16[304,1024]{1,0:T(8,128)(2,1)S(1)}, u32[]{:S(2)}, u32[]{:S(2)}) collective-permute-start(bf16[304,1024]{1,0:T(8,128)(2,1)S(1)} %add_convert_fusion.2), channel_id=1, source_target_pairs={{0,4},{4,8},{8,12},{12,14},{14,10},{10,6},{6,2},{2,0},{1,3},{5,1},... | collective-permute-start | bytes 1867784 | tf_op jit(solution)/shard_map/ppermute | solution.py:199
Sparse Core Ops, SparseCore 0:
  8.9 16.3 all-gather.5
  26.8 31.2 all-gather.7
  59.7 31.2 all-gather.9
where the time goes:
time: 321 us; the launch traced here: 317 us
  waiting for transfers between devices  107 us (33%)
  matrix products  53.6 us (17%)
  local copies, waits for them, and re-layouts  45.4 us (14%)
  starting transfers between devices  44.7 us (14%)
  between operations  34.8 us (11%)
  other arithmetic  28.2 us (9%)
  blocking collectives  3.64 us (1%)
    ppermute x14, waiting for transfers between devices, on_device(): acc[i] = lax.ppermute(send, both, ring_pairs)  74.9 us
    unnamed x74, local copies, waits for them, and re-layouts  37.6 us
    ppermute x14, waiting for transfers between devices, on_device(): moving[i] = lax.ppermute(moving[i], both, ring_pairs)  26.6 us
    ppermute x14, starting transfers between devices, on_device(): moving[i] = lax.ppermute(moving[i], both, ring_pairs)  21.2 us
    dot_general x2, matrix products, on_device(): jnp.dot(normed, query_full, preferred_element_type=jnp.float32)  18.4 us
    ppermute x14, starting transfers between devices, on_device(): acc[i] = lax.ppermute(send, both, ring_pairs)  18.1 us
    mul x2, other arithmetic, fast_prune(): weight.reshape(keep.shape[0], step_r, cols) * mask[:, None, :]  18 us
    dot_general x16, matrix products, chunk(): return jnp.dot(context, cols, preferred_element_type=jnp.float32)  13.3 us
  transfers between devices with their start and end apart: 35, of which 21 were waited for; matrix products, arithmetic and copies ran while one was open for 36% of the time, Pallas kernels for 0%

commit v1 on v0

--- a/solution.py
+++ b/solution.py
@@ -105,10 +105,8 @@
             lax.all_gather(query_keep, "dp", axis=0, tiled=True),
         )
         kv_full = lax.all_gather(kv_weight, "dp", axis=1, tiled=True)
-        out_full = fast_prune(
-            lax.all_gather(out_weight, "dp", axis=1, tiled=True),
-            lax.all_gather(out_keep, "dp", axis=1, tiled=True),
-        )
+        out_raw = lax.all_gather(out_weight, "dp", axis=1, tiled=True)
+        out_keep_full = lax.all_gather(out_keep, "dp", axis=1, tiled=True)
 
         split = (total_rows // 2 + 7) // 8 * 8
         moving = [hidden[:split], hidden[split:]]
@@ -177,17 +175,25 @@
             ).astype(jnp.bfloat16)
             return context.reshape(sizes[i], head_local * HD)
 
-        def chunk(context, dest_pos):
-            cols = lax.dynamic_slice_in_dim(out_full, ring[dest_pos % n] * feat, feat, axis=1)
-            return jnp.dot(context, cols, preferred_element_type=jnp.float32)
-
+        keep_step = out_raw.shape[1] // out_keep_full.shape[1]
+
+        def chunk_weight(dest_pos):
+            col = ring[dest_pos % n] * feat
+            cols = lax.dynamic_slice_in_dim(out_raw, col, feat, axis=1)
+            keep = lax.dynamic_slice_in_dim(out_keep_full, col // keep_step, feat // keep_step, axis=1)
+            return fast_prune(cols, keep)
+
+        weights_by_step = [chunk_weight(pos + sign * (n - 1 - s)) for s in range(n)]
         parts = []
         for i in range(2):
             q_rows = lax.slice_in_dim(queries, starts[i], starts[i] + sizes[i], axis=0)
             if i > 0:
                 q_rows, _ = lax.optimization_barrier((q_rows, parts[0][0]))
             context = context_rows(i, q_rows)
-            mine = [chunk(context, pos + sign * (n - 1 - s)) for s in range(n)]
+            mine = [
+                jnp.dot(context, weights_by_step[s], preferred_element_type=jnp.float32)
+                for s in range(n)
+            ]
             parts.append([mine[0].astype(jnp.bfloat16)] + lax.optimization_barrier(mine[1:]))
         acc = [None, None]
         for s in range(n - 1):

time: 321 us -> 330 us (1.028)
  matrix products: 53.6 us -> 59.8 us
  waiting for transfers between devices: 107 us -> 112 us
    ppermute x14, waiting for transfers between devices: 74.9 us -> 80.7 us  [on_device(): acc[i] = lax.ppermute(send, both, ring_pairs)]
    dot_general x2, matrix products: 12.9 us -> 18.1 us  [context_rows(): jnp.einsum('hqk,kd->qhd', probs, value_head, preferred_element_type=jnp.f...]
    ppermute x14, starting transfers between devices: 18.1 us -> 13.6 us  [on_device(): acc[i] = lax.ppermute(send, both, ring_pairs)]
    unnamed x74 -> x99, local copies, waits for them, and re-layouts: 37.6 us -> 36.1 us
  transfers between devices with their start and end apart: 35 -> 35, of which waited for: 21 -> 21; matrix products, arithmetic and copies ran while one was open for 36% -> 37% of each run, Pallas kernels for 0% -> 0%
where the time goes in v1:
time: 330 us; the launch traced here: 328 us
  waiting for transfers between devices  112 us (34%)
  matrix products  59.8 us (18%)
  local copies, waits for them, and re-layouts  48 us (15%)
  starting transfers between devices  42.3 us (13%)
  between operations  35.4 us (11%)
  other arithmetic  27.7 us (8%)
  blocking collectives  3.62 us (1%)
    ppermute x14, waiting for transfers between devices, on_device(): acc[i] = lax.ppermute(send, both, ring_pairs)  80.7 us
    unnamed x99, local copies, waits for them, and re-layouts  36.1 us
    ppermute x14, waiting for transfers between devices, on_device(): moving[i] = lax.ppermute(moving[i], both, ring_pairs)  26.4 us
    ppermute x14, starting transfers between devices, on_device(): moving[i] = lax.ppermute(moving[i], both, ring_pairs)  22.8 us
    dot_general x2, matrix products, on_device(): jnp.dot(normed, query_full, preferred_element_type=jnp.float32)  18.4 us
    dot_general x2, matrix products, context_rows(): jnp.einsum('hqk,kd->qhd', probs, value_head, preferred_element_type=jnp.f...  18.1 us
    mul x2, other arithmetic, fast_prune(): weight.reshape(keep.shape[0], step_r, cols) * mask[:, None, :]  17.7 us
    dot_general x16, matrix products, on_device(): jnp.dot(context, weights_by_step[s], preferred_element_type=jnp.float32)  14.3 us
  transfers between devices with their start and end apart: 35, of which 21 were waited for; matrix products, arithmetic and copies ran while one was open for 37% of the time, Pallas kernels for 0%

profile of v1, /device:TPU:0, one launch (start us, length us, event | category | flops | bytes accessed | tf_op | source)
XLA Modules:
  0.0 328.4 jit_solution(13196899079145729405)
XLA Ops:
  10.3 3.1 collective-permute-start.9
  14.2 1.6 collective-permute-start
  35.6 1.8 all-gather.1
  37.7 1.6 collective-permute-start.10
  40.8 1.5 collective-permute-start.1
  42.5 5.4 %collective-permute-done.10 = bf16[296,1024]{1,0:T(8,128)(2,1)} collective-permute-done((bf16[296,1024]{1,0:T(8,128)(2,1)S(1)}, bf16[296,1024]{1,0:T(8,128)(2,1)}, u32[]{:S(2)}, u32[]{:S(2)}) %collective-permute-start.10) | collective-permute-done | bytes 606240 | tf_op jit(solution)/shard_map/ppermute | solution.py:118
  47.9 1.6 collective-permute-start.11
  50.1 4.4 %collective-permute-done.1 = bf16[304,1024]{1,0:T(8,128)(2,1)S(1)} collective-permute-done((bf16[304,1024]{1,0:T(8,128)(2,1)S(1)}, bf16[304,1024]{1,0:T(8,128)(2,1)S(1)}, u32[]{:S(2)}, u32[]{:S(2)}) %collective-permute-start.1) | collective-permute-done | bytes 622624 | tf_op jit(solution)/shard_map/ppermute | solution.py:118
  54.5 1.6 collective-permute-start.2
  57.2 3.9 %collective-permute-done.11 = bf16[296,1024]{1,0:T(8,128)(2,1)} collective-permute-done((bf16[296,1024]{1,0:T(8,128)(2,1)}, bf16[296,1024]{1,0:T(8,128)(2,1)}, u32[]{:S(2)}, u32[]{:S(2)}) %collective-permute-start.11) | collective-permute-done | bytes 606240 | tf_op jit(solution)/shard_map/ppermute | solution.py:118
  61.1 1.6 collective-permute-start.12
  62.7 5.0 %collective-permute-done.2 = bf16[304,1024]{1,0:T(8,128)(2,1)S(1)} collective-permute-done((bf16[304,1024]{1,0:T(8,128)(2,1)S(1)}, bf16[304,1024]{1,0:T(8,128)(2,1)S(1)}, u32[]{:S(2)}, u32[]{:S(2)}) %collective-permute-start.2) | collective-permute-done | bytes 622624 | tf_op jit(solution)/shard_map/ppermute | solution.py:118
  67.7 1.6 collective-permute-start.3
  70.6 1.8 all-gather
  77.5 1.5 collective-permute-start.13
  79.1 2.0 constant_dynamic-update-slice_fusion.15
  81.1 1.3 collective-permute-start.4
  83.3 2.0 constant_dynamic-update-slice_fusion.14
  86.1 1.9 constant_dynamic-update-slice_fusion.13
  88.1 1.5 collective-permute-start.14
  90.4 4.1 %collective-permute-done.4 = bf16[304,1024]{1,0:T(8,128)(2,1)S(1)} collective-permute-done((bf16[304,1024]{1,0:T(8,128)(2,1)S(1)}, bf16[304,1024]{1,0:T(8,128)(2,1)S(1)}, u32[]{:S(2)}, u32[]{:S(2)}) %collective-permute-start.4) | collective-permute-done | bytes 622624 | tf_op jit(solution)/shard_map/ppermute | solution.py:118
  94.5 1.5 collective-permute-start.5
  96.0 2.0 constant_dynamic-update-slice_fusion.12
  101.1 1.5 collective-permute-start.15
  102.6 2.0 constant_dynamic-update-slice_fusion.10
  104.6 3.1 collective-permute-done.5
  107.7 1.5 collective-permute-start.6
  111.4 1.4 dynamic-slice_dynamic-update-slice_fusion.14
  120.5 2.6 fusion.22
  125.9 2.5 fusion.25
  128.4 3.6 %collective-permute-start.7 = (bf16[304,128]{0,1:T(8,128)(2,1)S(1)}, bf16[304,128]{0,1:T(8,128)(2,1)S(1)}, u32[]{:S(2)}, u32[]{:S(2)}) collective-permute-start(bf16[304,128]{0,1:T(8,128)(2,1)S(1)} %get-tuple-element.61), channel_id=1, source_target_pairs={{0,2},{2,6},{4,10},{6,14},{8,0},{10,4},{12,8},{14,12},{1,3},{3,7},... | collective-permute-start | bytes 233480 | tf_op jit(solution)/shard_map/ppermute | solution.py:151
  132.8 2.3 collective-permute-done.7
  136.0 9.8 %bitcast_multiply_fusion = bf16[8192,1024]{1,0:T(8,128)(2,1)S(1)} fusion(bf16[8192,1024]{1,0:T(8,128)(2,1)} %all-gather.8.cloned.1.call-done, bf16[128,1024]{1,0:T(8,128)(2,1)S(1)} %copy.38), kind=kLoop, calls=%fused_computation | loop fusion | flops 8388608 | bytes 33816576 | tf_op jit(solution)/shard_map/mul | solution.py:71
  145.8 1.5 dynamic-slice_dynamic-update-slice_fusion.7
  147.3 1.5 dynamic-slice_dynamic-update-slice_fusion.6
  148.8 1.5 dynamic-slice_dynamic-update-slice_fusion.5
  150.3 1.6 dynamic-slice_dynamic-update-slice_fusion.4
  151.8 1.5 dynamic-slice_dynamic-update-slice_fusion.3
  153.3 1.6 dynamic-slice_dynamic-update-slice_fusion.2
  154.9 1.5 dynamic-slice_dynamic-update-slice_fusion.1
  156.4 1.5 dynamic-slice_dynamic-update-slice_fusion
  157.9 9.4 %fusion.14 = f32[296,1024]{1,0:T(8,128)S(1)} fusion(bf16[8192,1024]{1,0:T(8,128)(2,1)} %dynamic-slice_dynamic-update-slice_fusion, bf16[296,8192]{1,0:T(8,128)(2,1)S(1)} %bitcast.181, f32[8192]{0:T(1024)S(1)} %copy-done.23, f32[296]{0:T(512)S(1)} %add_rsqrt_fusion), kind=kOutput, calls=%fused_computation.41 | convolution fusion | flops 4975755264 | bytes 22873248 | tf_op jit(solution)/shard_map/dot_general | solution.py:144
  167.3 9.0 %fusion.10 = f32[304,1024]{1,0:T(8,128)S(1)} fusion(bf16[8192,1024]{1,0:T(8,128)(2,1)} %dynamic-slice_dynamic-update-slice_fusion, bf16[304,8192]{1,0:T(8,128)(2,1)S(1)} %bitcast.179, f32[8192]{0:T(1024)S(1)} %copy-done.23, f32[304]{0:T(512)S(1)} %add_rsqrt_fusion.1), kind=kOutput, calls=%fused_computation.39 | convolution fusion | flops 5110235136 | bytes 23037120 | tf_op jit(solution)/shard_map/dot_general | solution.py:144
  179.2 2.0 fusion.6
  181.3 15.9 %fusion.20 = bf16[8,38,8,128]{3,2,1,0:T(8,128)(2,1)} fusion(f32[600,304,8]{0,1,2:T(8,128)S(1)} %get-tuple-element.93, f32[8,304]{1,0:T(8,128)S(1)} %get-tuple-element.92, pred[304,600]{1,0:T(8,128)(4,1)S(1)} %copy-done.5, bf16[296,128]{0,1:T(8,128)(2,1)S(1)} %get-tuple-element.59, bf16[304,128]{0,1:T(8,128)(2,1)S(1)} %get-tuple-element.57), kind=kOutput, calls=%fused_computation.47 | convolution fusion | flops 380010496 | bytes 6805120 | tf_op jit(solution)/shard_map/hqk,kd->qhd/dot_general | solution.py:173
  197.2 7.9 %bitcast_multiply_fusion.2 = (bf16[1024,1024]{1,0:T(8,128)(2,1)S(1)}, bf16[1024,1024]{1,0:T(8,128)(2,1)S(1)}, bf16[1024,1024]{1,0:T(8,128)(2,1)S(1)}, bf16[1024,...) fusion(bf16[1024,8192]{1,0:T(8,128)(2,1)} %all-gather.10.cloned, ...), kind=kLoop, calls=%fused_computation.23 | loop fusion | flops 33554432 | bytes 33816608 | tf_op jit(solution)/shard_map/mul | solution.py:71
  205.2 2.0 fusion.32
  208.0 5.5 %collective-permute-start.18 = (bf16[304,1024]{1,0:T(8,128)(2,1)S(1)}, bf16[304,1024]{1,0:T(8,128)(2,1)S(1)}, u32[]{:S(2)}, u32[]{:S(2)}) collective-permute-start(bf16[304,1024]{1,0:T(8,128)(2,1)S(1)} %convolution_convert_fusion), channel_id=1, source_target_pairs={{0,4},{4,8},{8,12},{12,14},{14,10},{10,6},{6,2},{2,0},{1,3},{5,1},... | collective-permute-start | bytes 1867784 | tf_op jit(solution)/shard_map/ppermute | solution.py:205
  213.5 1.9 fusion.7
  215.4 2.2 fusion.21
  229.3 8.3 %collective-permute-done.25 = bf16[296,1024]{1,0:T(8,128)(2,1)S(1)} collective-permute-done((bf16[296,1024]{1,0:T(8,128)(2,1)S(1)}, bf16[296,1024]{1,0:T(8,128)(2,1)S(1)}, u32[]{:S(2)}, u32[]{:S(2)}) %collective-permute-start.25) | collective-permute-done | bytes 606240 | tf_op jit(solution)/shard_map/ppermute | solution.py:205
  238.5 2.5 collective-permute-start.19
  241.0 6.9 %collective-permute-done.26 = bf16[296,1024]{1,0:T(8,128)(2,1)S(1)} collective-permute-done((bf16[296,1024]{1,0:T(8,128)(2,1)S(1)}, bf16[296,1024]{1,0:T(8,128)(2,1)S(1)}, u32[]{:S(2)}, u32[]{:S(2)}) %collective-permute-start.26) | collective-permute-done | bytes 606240 | tf_op jit(solution)/shard_map/ppermute | solution.py:205
  248.6 6.0 %collective-permute-done.19 = bf16[304,1024]{1,0:T(8,128)(2,1)S(1)} collective-permute-done((bf16[304,1024]{1,0:T(8,128)(2,1)S(1)}, bf16[304,1024]{1,0:T(8,128)(2,1)S(1)}, u32[]{:S(2)}, u32[]{:S(2)}) %collective-permute-start.19) | collective-permute-done | bytes 622624 | tf_op jit(solution)/shard_map/ppermute | solution.py:205
  255.3 5.8 %collective-permute-done.27 = bf16[296,1024]{1,0:T(8,128)(2,1)S(1)} collective-permute-done((bf16[296,1024]{1,0:T(8,128)(2,1)S(1)}, bf16[296,1024]{1,0:T(8,128)(2,1)S(1)}, u32[]{:S(2)}, u32[]{:S(2)}) %collective-permute-start.27) | collective-permute-done | bytes 606240 | tf_op jit(solution)/shard_map/ppermute | solution.py:205
  261.7 6.0 %collective-permute-done.20 = bf16[304,1024]{1,0:T(8,128)(2,1)S(1)} collective-permute-done((bf16[304,1024]{1,0:T(8,128)(2,1)S(1)}, bf16[304,1024]{1,0:T(8,128)(2,1)S(1)}, u32[]{:S(2)}, u32[]{:S(2)}) %collective-permute-start.20) | collective-permute-done | bytes 622624 | tf_op jit(solution)/shard_map/ppermute | solution.py:205
  268.4 5.8 %collective-permute-done.28 = bf16[296,1024]{1,0:T(8,128)(2,1)S(1)} collective-permute-done((bf16[296,1024]{1,0:T(8,128)(2,1)S(1)}, bf16[296,1024]{1,0:T(8,128)(2,1)S(1)}, u32[]{:S(2)}, u32[]{:S(2)}) %collective-permute-start.28) | collective-permute-done | bytes 606240 | tf_op jit(solution)/shard_map/ppermute | solution.py:205
  274.9 6.0 %collective-permute-done.21 = bf16[304,1024]{1,0:T(8,128)(2,1)S(1)} collective-permute-done((bf16[304,1024]{1,0:T(8,128)(2,1)S(1)}, bf16[304,1024]{1,0:T(8,128)(2,1)S(1)}, u32[]{:S(2)}, u32[]{:S(2)}) %collective-permute-start.21) | collective-permute-done | bytes 622624 | tf_op jit(solution)/shard_map/ppermute | solution.py:205
  281.6 5.8 %collective-permute-done.29 = bf16[296,1024]{1,0:T(8,128)(2,1)S(1)} collective-permute-done((bf16[296,1024]{1,0:T(8,128)(2,1)S(1)}, bf16[296,1024]{1,0:T(8,128)(2,1)S(1)}, u32[]{:S(2)}, u32[]{:S(2)}) %collective-permute-start.29) | collective-permute-done | bytes 606240 | tf_op jit(solution)/shard_map/ppermute | solution.py:205
  288.1 6.0 %collective-permute-done.22 = bf16[304,1024]{1,0:T(8,128)(2,1)S(1)} collective-permute-done((bf16[304,1024]{1,0:T(8,128)(2,1)S(1)}, bf16[304,1024]{1,0:T(8,128)(2,1)S(1)}, u32[]{:S(2)}, u32[]{:S(2)}) %collective-permute-start.22) | collective-permute-done | bytes 622624 | tf_op jit(solution)/shard_map/ppermute | solution.py:205
  294.8 5.8 %collective-permute-done.30 = bf16[296,1024]{1,0:T(8,128)(2,1)S(1)} collective-permute-done((bf16[296,1024]{1,0:T(8,128)(2,1)S(1)}, bf16[296,1024]{1,0:T(8,128)(2,1)S(1)}, u32[]{:S(2)}, u32[]{:S(2)}) %collective-permute-start.30) | collective-permute-done | bytes 606240 | tf_op jit(solution)/shard_map/ppermute | solution.py:205
  301.2 6.0 %collective-permute-done.23 = bf16[304,1024]{1,0:T(8,128)(2,1)S(1)} collective-permute-done((bf16[304,1024]{1,0:T(8,128)(2,1)S(1)}, bf16[304,1024]{1,0:T(8,128)(2,1)S(1)}, u32[]{:S(2)}, u32[]{:S(2)}) %collective-permute-start.23) | collective-permute-done | bytes 622624 | tf_op jit(solution)/shard_map/ppermute | solution.py:205
  307.9 5.8 %collective-permute-done.31 = bf16[296,1024]{1,0:T(8,128)(2,1)S(1)} collective-permute-done((bf16[296,1024]{1,0:T(8,128)(2,1)S(1)}, bf16[296,1024]{1,0:T(8,128)(2,1)S(1)}, u32[]{:S(2)}, u32[]{:S(2)}) %collective-permute-start.31) | collective-permute-done | bytes 606240 | tf_op jit(solution)/shard_map/ppermute | solution.py:205
  313.9 6.5 %collective-permute-done.24 = bf16[304,1024]{1,0:T(8,128)(2,1)S(1)} collective-permute-done((bf16[304,1024]{1,0:T(8,128)(2,1)S(1)}, bf16[304,1024]{1,0:T(8,128)(2,1)S(1)}, u32[]{:S(2)}, u32[]{:S(2)}) %collective-permute-start.24) | collective-permute-done | bytes 622624 | tf_op jit(solution)/shard_map/ppermute | solution.py:205
  (211 shorter events, 57.4 us)
Async XLA Ops:
  6.5 103.6 %all-gather.6.cloned.1.call-start = ((), (), s32[]{:S(2)}) async-start(), calls=%async_computation | async-start | bytes 6291456 | tf_op jit(solution)/shard_map/all_gather | solution.py:107
  7.3 128.7 %all-gather.8.cloned.1.call-start = ((), (), s32[]{:S(2)}) async-start(), calls=%async_computation.1 | async-start | bytes 25165824 | tf_op jit(solution)/shard_map/all_gather | solution.py:104
  8.0 7.8 %copy-start.24 = (s32[8]{0:T(128)S(1)}, s32[8]{0:T(128)}, u32[]{:S(2)}) copy-start(s32[8]{0:T(128)} %constant.213.clone) | copy-start | bytes 100
  8.0 19.7 %copy-start.10 = (s32[8]{0:T(128)S(1)}, s32[8]{0:T(128)}, u32[]{:S(2)}) copy-start(s32[8]{0:T(128)} %constant.214.clone) | copy-start | bytes 100
  8.0 189.2 %all-gather.10.cloned.1.call-start = ((), (), s32[]{:S(2)}) async-start(), calls=%async_computation.2 | async-start | bytes 25165824 | tf_op jit(solution)/shard_map/all_gather | solution.py:108
  9.3 26.3 %copy-start.18 = (s32[16,64]{1,0:T(8,128)S(1)}, s32[16,64]{1,0:T(8,128)}, u32[]{:S(2)}) copy-start(s32[16,64]{1,0:T(8,128)} %param.17) | copy-start | bytes 12292
  9.3 28.2 %copy-start.17 = (f32[8192]{0:T(1024)S(1)}, f32[8192]{0:T(1024)}, u32[]{:S(2)}) copy-start(f32[8192]{0:T(1024)} %param.12) | copy-start | bytes 98308
  9.3 31.3 %copy-start.20 = (s32[1,4]{1,0:T(1,128)S(1)}, s32[1,4]{1,0:T(1,128)}, u32[]{:S(2)}) copy-start(s32[1,4]{1,0:T(1,128)} %param.18) | copy-start | bytes 52
  9.3 33.1 %copy-start.21 = (s32[1,4]{1,0:T(1,128)S(1)}, s32[1,4]{1,0:T(1,128)}, u32[]{:S(2)}) copy-start(s32[1,4]{1,0:T(1,128)} %param.19) | copy-start | bytes 52
  9.3 61.3 %copy-start.19 = (s32[64,16]{0,1:T(8,128)S(1)}, s32[64,16]{0,1:T(8,128)}, u32[]{:S(2)}) copy-start(s32[64,16]{0,1:T(8,128)} %param.14) | copy-start | bytes 12292
  10.3 27.4 %collective-permute-start.9 = (bf16[296,1024]{1,0:T(8,128)(2,1)S(1)}, bf16[296,1024]{1,0:T(8,128)(2,1)S(1)}, u32[]{:S(2)}, u32[]{:S(2)}) collective-permute-start(bf16[296,1024]{1,0:T(8,128)(2,1)S(1)} %get-tuple-element.53), channel_id=1, source_target_pairs={{0,4},{4,8},{8,12},{12,14},{14,10},{10,6},{6,2},{2,0},{1,3},{5,1},... | collective-permute-start | bytes 1818632 | tf_op jit(solution)/shard_map/ppermute | solution.py:118
  14.2 26.6 %collective-permute-start = (bf16[304,1024]{1,0:T(8,128)(2,1)S(1)}, bf16[304,1024]{1,0:T(8,128)(2,1)S(1)}, u32[]{:S(2)}, u32[]{:S(2)}) collective-permute-start(bf16[304,1024]{1,0:T(8,128)(2,1)S(1)} %get-tuple-element.51), channel_id=1, source_target_pairs={{0,4},{4,8},{8,12},{12,14},{14,10},{10,6},{6,2},{2,0},{1,3},{5,1},... | collective-permute-start | bytes 1867784 | tf_op jit(solution)/shard_map/ppermute | solution.py:118
  37.7 12.4 %copy-start.4 = (bf16[296,1024]{1,0:T(8,128)(2,1)}, bf16[296,1024]{1,0:T(8,128)(2,1)S(1)}, u32[]{:S(2)}) copy-start(bf16[296,1024]{1,0:T(8,128)(2,1)S(1)} %collective-permute-done.9) | copy-start | bytes 1818628
  37.7 10.2 %collective-permute-start.10 = (bf16[296,1024]{1,0:T(8,128)(2,1)S(1)}, bf16[296,1024]{1,0:T(8,128)(2,1)}, u32[]{:S(2)}, u32[]{:S(2)}) collective-permute-start(bf16[296,1024]{1,0:T(8,128)(2,1)S(1)} %collective-permute-done.9), channel_id=1, source_target_pairs={{0,4},{4,8},{8,12},{12,14},{14,10},{10,6},{6,2},{2,0},{1,3},{5,1},... | collective-permute-start | bytes 1818632 | tf_op jit(solution)/shard_map/ppermute | solution.py:118
  40.8 13.7 %collective-permute-start.1 = (bf16[304,1024]{1,0:T(8,128)(2,1)S(1)}, bf16[304,1024]{1,0:T(8,128)(2,1)S(1)}, u32[]{:S(2)}, u32[]{:S(2)}) collective-permute-start(bf16[304,1024]{1,0:T(8,128)(2,1)S(1)} %collective-permute-done), channel_id=1, source_target_pairs={{0,4},{4,8},{8,12},{12,14},{14,10},{10,6},{6,2},{2,0},{1,3},{5,1},... | collective-permute-start | bytes 1867784 | tf_op jit(solution)/shard_map/ppermute | solution.py:118
  47.9 13.2 %collective-permute-start.11 = (bf16[296,1024]{1,0:T(8,128)(2,1)}, bf16[296,1024]{1,0:T(8,128)(2,1)}, u32[]{:S(2)}, u32[]{:S(2)}) collective-permute-start(bf16[296,1024]{1,0:T(8,128)(2,1)} %collective-permute-done.10), channel_id=1, source_target_pairs={{0,4},{4,8},{8,12},{12,14},{14,10},{10,6},{6,2},{2,0},{1,3},{5,1},... | collective-permute-start | bytes 1818632 | tf_op jit(solution)/shard_map/ppermute | solution.py:118
  54.5 13.2 %collective-permute-start.2 = (bf16[304,1024]{1,0:T(8,128)(2,1)S(1)}, bf16[304,1024]{1,0:T(8,128)(2,1)S(1)}, u32[]{:S(2)}, u32[]{:S(2)}) collective-permute-start(bf16[304,1024]{1,0:T(8,128)(2,1)S(1)} %collective-permute-done.1), channel_id=1, source_target_pairs={{0,4},{4,8},{8,12},{12,14},{14,10},{10,6},{6,2},{2,0},{1,3},{5,1},... | collective-permute-start | bytes 1867784 | tf_op jit(solution)/shard_map/ppermute | solution.py:118
  61.1 16.4 %collective-permute-start.12 = (bf16[296,1024]{1,0:T(8,128)(2,1)}, bf16[296,1024]{1,0:T(8,128)(2,1)}, u32[]{:S(2)}, u32[]{:S(2)}) collective-permute-start(bf16[296,1024]{1,0:T(8,128)(2,1)} %collective-permute-done.11), channel_id=1, source_target_pairs={{0,4},{4,8},{8,12},{12,14},{14,10},{10,6},{6,2},{2,0},{1,3},{5,1},... | collective-permute-start | bytes 1818632 | tf_op jit(solution)/shard_map/ppermute | solution.py:118
  62.7 13.7 %copy-start.22 = (f32[8192]{0:T(1024)}, f32[8192]{0:T(1024)S(1)}, u32[]{:S(2)}) copy-start(f32[8192]{0:T(1024)S(1)} %constant_dynamic-update-slice_fusion.17) | copy-start | bytes 98308
  67.7 13.4 %collective-permute-start.3 = (bf16[304,1024]{1,0:T(8,128)(2,1)S(1)}, bf16[304,1024]{1,0:T(8,128)(2,1)S(1)}, u32[]{:S(2)}, u32[]{:S(2)}) collective-permute-start(bf16[304,1024]{1,0:T(8,128)(2,1)S(1)} %collective-permute-done.2), channel_id=1, source_target_pairs={{0,4},{4,8},{8,12},{12,14},{14,10},{10,6},{6,2},{2,0},{1,3},{5,1},... | collective-permute-start | bytes 1867784 | tf_op jit(solution)/shard_map/ppermute | solution.py:118
  77.5 10.5 %collective-permute-start.13 = (bf16[296,1024]{1,0:T(8,128)(2,1)}, bf16[296,1024]{1,0:T(8,128)(2,1)S(1)}, u32[]{:S(2)}, u32[]{:S(2)}) collective-permute-start(bf16[296,1024]{1,0:T(8,128)(2,1)} %collective-permute-done.12), channel_id=1, source_target_pairs={{0,4},{4,8},{8,12},{12,14},{14,10},{10,6},{6,2},{2,0},{1,3},{5,1},... | collective-permute-start | bytes 1818632 | tf_op jit(solution)/shard_map/ppermute | solution.py:118
  81.1 13.4 %collective-permute-start.4 = (bf16[304,1024]{1,0:T(8,128)(2,1)S(1)}, bf16[304,1024]{1,0:T(8,128)(2,1)S(1)}, u32[]{:S(2)}, u32[]{:S(2)}) collective-permute-start(bf16[304,1024]{1,0:T(8,128)(2,1)S(1)} %collective-permute-done.3), channel_id=1, source_target_pairs={{0,4},{4,8},{8,12},{12,14},{14,10},{10,6},{6,2},{2,0},{1,3},{5,1},... | collective-permute-start | bytes 1867784 | tf_op jit(solution)/shard_map/ppermute | solution.py:118
  88.1 13.1 %collective-permute-start.14 = (bf16[296,1024]{1,0:T(8,128)(2,1)S(1)}, bf16[296,1024]{1,0:T(8,128)(2,1)}, u32[]{:S(2)}, u32[]{:S(2)}) collective-permute-start(bf16[296,1024]{1,0:T(8,128)(2,1)S(1)} %collective-permute-done.13), channel_id=1, source_target_pairs={{0,4},{4,8},{8,12},{12,14},{14,10},{10,6},{6,2},{2,0},{1,3},{5,1},... | collective-permute-start | bytes 1818632 | tf_op jit(solution)/shard_map/ppermute | solution.py:118
  94.5 13.2 %collective-permute-start.5 = (bf16[304,1024]{1,0:T(8,128)(2,1)S(1)}, bf16[304,1024]{1,0:T(8,128)(2,1)S(1)}, u32[]{:S(2)}, u32[]{:S(2)}) collective-permute-start(bf16[304,1024]{1,0:T(8,128)(2,1)S(1)} %collective-permute-done.4), channel_id=1, source_target_pairs={{0,4},{4,8},{8,12},{12,14},{14,10},{10,6},{6,2},{2,0},{1,3},{5,1},... | collective-permute-start | bytes 1867784 | tf_op jit(solution)/shard_map/ppermute | solution.py:118
  101.1 18.2 %collective-permute-start.15 = (bf16[296,1024]{1,0:T(8,128)(2,1)}, bf16[296,1024]{1,0:T(8,128)(2,1)S(1)}, u32[]{:S(2)}, u32[]{:S(2)}) collective-permute-start(bf16[296,1024]{1,0:T(8,128)(2,1)} %collective-permute-done.14), channel_id=1, source_target_pairs={{0,4},{4,8},{8,12},{12,14},{14,10},{10,6},{6,2},{2,0},{1,3},{5,1},... | collective-permute-start | bytes 1818632 | tf_op jit(solution)/shard_map/ppermute | solution.py:118
  107.7 17.0 %collective-permute-start.6 = (bf16[304,1024]{1,0:T(8,128)(2,1)S(1)}, bf16[304,1024]{1,0:T(8,128)(2,1)S(1)}, u32[]{:S(2)}, u32[]{:S(2)}) collective-permute-start(bf16[304,1024]{1,0:T(8,128)(2,1)S(1)} %collective-permute-done.5), channel_id=1, source_target_pairs={{0,4},{4,8},{8,12},{12,14},{14,10},{10,6},{6,2},{2,0},{1,3},{5,1},... | collective-permute-start | bytes 1867784 | tf_op jit(solution)/shard_map/ppermute | solution.py:118
  110.2 9.2 %copy-start.1 = (bf16[296,8192]{1,0:T(8,128)(2,1)S(1)}, bf16[296,8192]{1,0:T(8,128)(2,1)}, u32[]{:S(2)}) copy-start(bf16[296,8192]{1,0:T(8,128)(2,1)} %constant_dynamic-update-slice_fusion.10) | copy-start | bytes 14548996
  117.1 3.3 %copy-start.23 = (f32[8192]{0:T(1024)S(1)}, f32[8192]{0:T(1024)}, u32[]{:S(2)}) copy-start(f32[8192]{0:T(1024)} %copy-done.22) | copy-start | bytes 98308
  119.4 3.7 %copy-start.2 = (bf16[296,8192]{1,0:T(8,128)(2,1)}, bf16[296,8192]{1,0:T(8,128)(2,1)S(1)}, u32[]{:S(2)}) copy-start(bf16[296,8192]{1,0:T(8,128)(2,1)S(1)} %constant_dynamic-update-slice_fusion.9) | copy-start | bytes 14548996
  119.4 5.3 %slice-start = ((s8[4980736]{0:T(1024)(128)(4,1)}), s8[4194304]{0:T(1024)(128)(4,1)S(1)}, s32[]{:S(2)}) async-start(s8[4980736]{0:T(1024)(128)(4,1)} %bitcast.176), calls=%async_computation.3 | async-start | bytes 8388608
  120.5 4.2 %slice-start.1 = ((s8[4980736]{0:T(1024)(128)(4,1)}), s8[786432]{0:T(1024)(128)(4,1)S(1)}, s32[]{:S(2)}) async-start(s8[4980736]{0:T(1024)(128)(4,1)} %bitcast.176), calls=%async_computation.4 | async-start | bytes 1572864
  123.2 9.5 %collective-permute-start.16 = (bf16[296,128]{0,1:T(8,128)(2,1)S(1)}, bf16[296,128]{0,1:T(8,128)(2,1)S(1)}, u32[]{:S(2)}, u32[]{:S(2)}) collective-permute-start(bf16[296,128]{0,1:T(8,128)(2,1)S(1)} %get-tuple-element.63), channel_id=1, source_target_pairs={{0,2},{2,6},{4,10},{6,14},{8,0},{10,4},{12,8},{14,12},{1,3},{3,7},... | collective-permute-start | bytes 227336 | tf_op jit(solution)/shard_map/ppermute | solution.py:151
  123.8 9.0 %collective-permute-start.17 = (bf16[296,128]{0,1:T(8,128)(2,1)S(1)}, bf16[296,128]{0,1:T(8,128)(2,1)S(1)}, u32[]{:S(2)}, u32[]{:S(2)}) collective-permute-start(bf16[296,128]{0,1:T(8,128)(2,1)S(1)} %get-tuple-element.64), channel_id=1, source_target_pairs={{0,0},{2,4},{4,8},{6,12},{8,2},{10,6},{12,10},{14,14},{1,1},{3,5},... | collective-permute-start | bytes 227336 | tf_op jit(solution)/shard_map/ppermute | solution.py:150
  124.8 3.6 %copy-start = (bf16[304,8192]{1,0:T(8,128)(2,1)}, bf16[304,8192]{1,0:T(8,128)(2,1)S(1)}, u32[]{:S(2)}) copy-start(bf16[304,8192]{1,0:T(8,128)(2,1)S(1)} %constant_dynamic-update-slice_fusion) | copy-start | bytes 14942212
  128.4 6.7 %collective-permute-start.7 = (bf16[304,128]{0,1:T(8,128)(2,1)S(1)}, bf16[304,128]{0,1:T(8,128)(2,1)S(1)}, u32[]{:S(2)}, u32[]{:S(2)}) collective-permute-start(bf16[304,128]{0,1:T(8,128)(2,1)S(1)} %get-tuple-element.61), channel_id=1, source_target_pairs={{0,2},{2,6},{4,10},{6,14},{8,0},{10,4},{12,8},{14,12},{1,3},{3,7},... | collective-permute-start | bytes 233480 | tf_op jit(solution)/shard_map/ppermute | solution.py:151
  132.0 3.1 collective-permute-start.8
  135.1 46.1 %copy-start.11 = (bf16[304,128]{0,1:T(8,128)(2,1)}, bf16[304,128]{0,1:T(8,128)(2,1)S(1)}, u32[]{:S(2)}) copy-start(bf16[304,128]{0,1:T(8,128)(2,1)S(1)} %get-tuple-element.57) | copy-start | bytes 233476
  135.9 43.2 %copy-start.13 = (bf16[600,1,64]{0,2,1:T(8,128)(2,1)}, bf16[600,1,64]{0,2,1:T(8,128)(2,1)S(1)}, u32[]{:S(2)}) copy-start(bf16[600,1,64]{0,2,1:T(8,128)(2,1)S(1)} %get-tuple-element.55) | copy-start | bytes 230404
  135.9 43.2 %copy-start.15 = (bf16[600,1,64]{0,2,1:T(8,128)(2,1)}, bf16[600,1,64]{0,2,1:T(8,128)(2,1)S(1)}, u32[]{:S(2)}) copy-start(bf16[600,1,64]{0,2,1:T(8,128)(2,1)S(1)} %get-tuple-element.56) | copy-start | bytes 230404
  153.3 4.5 %slice-start.4 = ((s8[4849664]{0:T(1024)(128)(4,1)}), s8[4194304]{0:T(1024)(128)(4,1)S(1)}, s32[]{:S(2)}) async-start(s8[4849664]{0:T(1024)(128)(4,1)} %bitcast.180), calls=%async_computation.7 | async-start | bytes 8388608
  154.9 2.9 slice-start.5
  156.4 10.9 %slice-start.2 = ((s8[4980736]{0:T(1024)(128)(4,1)}), s8[4194304]{0:T(1024)(128)(4,1)S(1)}, s32[]{:S(2)}) async-start(s8[4980736]{0:T(1024)(128)(4,1)} %bitcast.178), calls=%async_computation.5 | async-start | bytes 8388608
  157.9 9.4 %slice-start.3 = ((s8[4980736]{0:T(1024)(128)(4,1)}), s8[786432]{0:T(1024)(128)(4,1)S(1)}, s32[]{:S(2)}) async-start(s8[4980736]{0:T(1024)(128)(4,1)} %bitcast.178), calls=%async_computation.6 | async-start | bytes 1572864
  181.3 15.9 %copy-start.7 = (bf16[16,1024]{1,0:T(8,128)(2,1)S(1)}, bf16[16,1024]{1,0:T(8,128)(2,1)}, u32[]{:S(2)}) copy-start(bf16[16,1024]{1,0:T(8,128)(2,1)} %mul.499) | copy-start | bytes 98308
  181.3 15.9 %copy-start.8 = (bf16[16,1024]{1,0:T(8,128)(2,1)S(1)}, bf16[16,1024]{1,0:T(8,128)(2,1)}, u32[]{:S(2)}) copy-start(bf16[16,1024]{1,0:T(8,128)(2,1)} %mul.505) | copy-start | bytes 98308
  181.3 15.9 %copy-start.9 = (bf16[16,1024]{1,0:T(8,128)(2,1)S(1)}, bf16[16,1024]{1,0:T(8,128)(2,1)}, u32[]{:S(2)}) copy-start(bf16[16,1024]{1,0:T(8,128)(2,1)} %mul.511) | copy-start | bytes 98308
  205.1 8.4 %copy-start.6 = (pred[296,600]{1,0:T(8,128)(4,1)S(1)}, pred[296,600]{1,0:T(8,128)(4,1)}, u32[]{:S(2)}) copy-start(pred[296,600]{1,0:T(8,128)(4,1)} %slice.67) | copy-start | bytes 532804
  205.1 8.3 %copy-start.14 = (bf16[600,1,64]{0,2,1:T(8,128)(2,1)S(1)}, bf16[600,1,64]{0,2,1:T(8,128)(2,1)}, u32[]{:S(2)}) copy-start(bf16[600,1,64]{0,2,1:T(8,128)(2,1)} %copy-done.13) | copy-start | bytes 230404
  205.2 8.3 %copy-start.16 = (bf16[600,1,64]{0,2,1:T(8,128)(2,1)S(1)}, bf16[600,1,64]{0,2,1:T(8,128)(2,1)}, u32[]{:S(2)}) copy-start(bf16[600,1,64]{0,2,1:T(8,128)(2,1)} %copy-done.15) | copy-start | bytes 230404
  208.0 7.4 %copy-start.12 = (bf16[304,128]{0,1:T(8,128)(2,1)S(1)}, bf16[304,128]{0,1:T(8,128)(2,1)}, u32[]{:S(2)}) copy-start(bf16[304,128]{0,1:T(8,128)(2,1)} %copy-done.11) | copy-start | bytes 233476
  208.0 30.3 %collective-permute-start.18 = (bf16[304,1024]{1,0:T(8,128)(2,1)S(1)}, bf16[304,1024]{1,0:T(8,128)(2,1)S(1)}, u32[]{:S(2)}, u32[]{:S(2)}) collective-permute-start(bf16[304,1024]{1,0:T(8,128)(2,1)S(1)} %convolution_convert_fusion), channel_id=1, source_target_pairs={{0,4},{4,8},{8,12},{12,14},{14,10},{10,6},{6,2},{2,0},{1,3},{5,1},... | collective-permute-start | bytes 1867784 | tf_op jit(solution)/shard_map/ppermute | solution.py:205
  227.5 10.1 %collective-permute-start.25 = (bf16[296,1024]{1,0:T(8,128)(2,1)S(1)}, bf16[296,1024]{1,0:T(8,128)(2,1)S(1)}, u32[]{:S(2)}, u32[]{:S(2)}) collective-permute-start(bf16[296,1024]{1,0:T(8,128)(2,1)S(1)} %convolution_convert_fusion.1), channel_id=1, source_target_pairs={{0,4},{4,8},{8,12},{12,14},{14,10},{10,6},{6,2},{2,0},{1,3},{5,1},... | collective-permute-start | bytes 1818632 | tf_op jit(solution)/shard_map/ppermute | solution.py:205
  237.8 10.1 %collective-permute-start.26 = (bf16[296,1024]{1,0:T(8,128)(2,1)S(1)}, bf16[296,1024]{1,0:T(8,128)(2,1)S(1)}, u32[]{:S(2)}, u32[]{:S(2)}) collective-permute-start(bf16[296,1024]{1,0:T(8,128)(2,1)S(1)} %add_convert_fusion.14), channel_id=1, source_target_pairs={{0,4},{4,8},{8,12},{12,14},{14,10},{10,6},{6,2},{2,0},{1,3},{5,1},... | collective-permute-start | bytes 1818632 | tf_op jit(solution)/shard_map/ppermute | solution.py:205
  238.5 16.1 %collective-permute-start.19 = (bf16[304,1024]{1,0:T(8,128)(2,1)S(1)}, bf16[304,1024]{1,0:T(8,128)(2,1)S(1)}, u32[]{:S(2)}, u32[]{:S(2)}) collective-permute-start(bf16[304,1024]{1,0:T(8,128)(2,1)S(1)} %add_convert_fusion.7), channel_id=1, source_target_pairs={{0,4},{4,8},{8,12},{12,14},{14,10},{10,6},{6,2},{2,0},{1,3},{5,1},... | collective-permute-start | bytes 1867784 | tf_op jit(solution)/shard_map/ppermute | solution.py:205
  248.1 13.0 %collective-permute-start.27 = (bf16[296,1024]{1,0:T(8,128)(2,1)S(1)}, bf16[296,1024]{1,0:T(8,128)(2,1)S(1)}, u32[]{:S(2)}, u32[]{:S(2)}) collective-permute-start(bf16[296,1024]{1,0:T(8,128)(2,1)S(1)} %add_convert_fusion.13), channel_id=1, source_target_pairs={{0,4},{4,8},{8,12},{12,14},{14,10},{10,6},{6,2},{2,0},{1,3},{5,1},... | collective-permute-start | bytes 1818632 | tf_op jit(solution)/shard_map/ppermute | solution.py:205
  254.8 13.0 %collective-permute-start.20 = (bf16[304,1024]{1,0:T(8,128)(2,1)S(1)}, bf16[304,1024]{1,0:T(8,128)(2,1)S(1)}, u32[]{:S(2)}, u32[]{:S(2)}) collective-permute-start(bf16[304,1024]{1,0:T(8,128)(2,1)S(1)} %add_convert_fusion.6), channel_id=1, source_target_pairs={{0,4},{4,8},{8,12},{12,14},{14,10},{10,6},{6,2},{2,0},{1,3},{5,1},... | collective-permute-start | bytes 1867784 | tf_op jit(solution)/shard_map/ppermute | solution.py:205
  261.2 13.0 %collective-permute-start.28 = (bf16[296,1024]{1,0:T(8,128)(2,1)S(1)}, bf16[296,1024]{1,0:T(8,128)(2,1)S(1)}, u32[]{:S(2)}, u32[]{:S(2)}) collective-permute-start(bf16[296,1024]{1,0:T(8,128)(2,1)S(1)} %add_convert_fusion.12), channel_id=1, source_target_pairs={{0,4},{4,8},{8,12},{12,14},{14,10},{10,6},{6,2},{2,0},{1,3},{5,1},... | collective-permute-start | bytes 1818632 | tf_op jit(solution)/shard_map/ppermute | solution.py:205
  267.9 13.0 %collective-permute-start.21 = (bf16[304,1024]{1,0:T(8,128)(2,1)S(1)}, bf16[304,1024]{1,0:T(8,128)(2,1)S(1)}, u32[]{:S(2)}, u32[]{:S(2)}) collective-permute-start(bf16[304,1024]{1,0:T(8,128)(2,1)S(1)} %add_convert_fusion.5), channel_id=1, source_target_pairs={{0,4},{4,8},{8,12},{12,14},{14,10},{10,6},{6,2},{2,0},{1,3},{5,1},... | collective-permute-start | bytes 1867784 | tf_op jit(solution)/shard_map/ppermute | solution.py:205
  274.4 13.0 %collective-permute-start.29 = (bf16[296,1024]{1,0:T(8,128)(2,1)S(1)}, bf16[296,1024]{1,0:T(8,128)(2,1)S(1)}, u32[]{:S(2)}, u32[]{:S(2)}) collective-permute-start(bf16[296,1024]{1,0:T(8,128)(2,1)S(1)} %add_convert_fusion.11), channel_id=1, source_target_pairs={{0,4},{4,8},{8,12},{12,14},{14,10},{10,6},{6,2},{2,0},{1,3},{5,1},... | collective-permute-start | bytes 1818632 | tf_op jit(solution)/shard_map/ppermute | solution.py:205
  281.1 13.0 %collective-permute-start.22 = (bf16[304,1024]{1,0:T(8,128)(2,1)S(1)}, bf16[304,1024]{1,0:T(8,128)(2,1)S(1)}, u32[]{:S(2)}, u32[]{:S(2)}) collective-permute-start(bf16[304,1024]{1,0:T(8,128)(2,1)S(1)} %add_convert_fusion.4), channel_id=1, source_target_pairs={{0,4},{4,8},{8,12},{12,14},{14,10},{10,6},{6,2},{2,0},{1,3},{5,1},... | collective-permute-start | bytes 1867784 | tf_op jit(solution)/shard_map/ppermute | solution.py:205
  287.6 13.0 %collective-permute-start.30 = (bf16[296,1024]{1,0:T(8,128)(2,1)S(1)}, bf16[296,1024]{1,0:T(8,128)(2,1)S(1)}, u32[]{:S(2)}, u32[]{:S(2)}) collective-permute-start(bf16[296,1024]{1,0:T(8,128)(2,1)S(1)} %add_convert_fusion.10), channel_id=1, source_target_pairs={{0,4},{4,8},{8,12},{12,14},{14,10},{10,6},{6,2},{2,0},{1,3},{5,1},... | collective-permute-start | bytes 1818632 | tf_op jit(solution)/shard_map/ppermute | solution.py:205
  294.3 13.0 %collective-permute-start.23 = (bf16[304,1024]{1,0:T(8,128)(2,1)S(1)}, bf16[304,1024]{1,0:T(8,128)(2,1)S(1)}, u32[]{:S(2)}, u32[]{:S(2)}) collective-permute-start(bf16[304,1024]{1,0:T(8,128)(2,1)S(1)} %add_convert_fusion.3), channel_id=1, source_target_pairs={{0,4},{4,8},{8,12},{12,14},{14,10},{10,6},{6,2},{2,0},{1,3},{5,1},... | collective-permute-start | bytes 1867784 | tf_op jit(solution)/shard_map/ppermute | solution.py:205
  300.7 13.0 %collective-permute-start.31 = (bf16[296,1024]{1,0:T(8,128)(2,1)S(1)}, bf16[296,1024]{1,0:T(8,128)(2,1)S(1)}, u32[]{:S(2)}, u32[]{:S(2)}) collective-permute-start(bf16[296,1024]{1,0:T(8,128)(2,1)S(1)} %add_convert_fusion.9), channel_id=1, source_target_pairs={{0,4},{4,8},{8,12},{12,14},{14,10},{10,6},{6,2},{2,0},{1,3},{5,1},... | collective-permute-start | bytes 1818632 | tf_op jit(solution)/shard_map/ppermute | solution.py:205
  307.4 13.0 %collective-permute-start.24 = (bf16[304,1024]{1,0:T(8,128)(2,1)S(1)}, bf16[304,1024]{1,0:T(8,128)(2,1)S(1)}, u32[]{:S(2)}, u32[]{:S(2)}) collective-permute-start(bf16[304,1024]{1,0:T(8,128)(2,1)S(1)} %add_convert_fusion.2), channel_id=1, source_target_pairs={{0,4},{4,8},{8,12},{12,14},{14,10},{10,6},{6,2},{2,0},{1,3},{5,1},... | collective-permute-start | bytes 1867784 | tf_op jit(solution)/shard_map/ppermute | solution.py:205
  (3 other events, 4.7 us)
Sparse Core Ops, SparseCore 0:
  8.9 16.3 all-gather.5
  26.8 31.2 all-gather.7
  59.7 31.2 all-gather.9

commit v2 on v0

--- a/solution.py
+++ b/solution.py
@@ -100,10 +100,17 @@
         total_rows, feat = hidden.shape
         head_local = query_weight.shape[1] // HD
 
-        query_full = fast_prune(
-            lax.all_gather(query_weight, "dp", axis=0, tiled=True),
-            lax.all_gather(query_keep, "dp", axis=0, tiled=True),
-        )
+        swap = [(0, 1), (1, 0)]
+
+        def full_over_dp(local, axis):
+            other = lax.ppermute(local, "dp", swap)
+            return jnp.where(
+                dp_rank == 0,
+                jnp.concatenate([local, other], axis=axis),
+                jnp.concatenate([other, local], axis=axis),
+            )
+
+        query_full = fast_prune(full_over_dp(query_weight, 0), full_over_dp(query_keep, 0))
         kv_full = lax.all_gather(kv_weight, "dp", axis=1, tiled=True)
         out_full = fast_prune(
             lax.all_gather(out_weight, "dp", axis=1, tiled=True),

time: 321 us -> 323 us (level)
    ppermute x14, waiting for transfers between devices: 74.9 us -> 79.7 us  [on_device(): acc[i] = lax.ppermute(send, both, ring_pairs)]
    ppermute x14, starting transfers between devices: 18.1 us -> 14.4 us  [on_device(): acc[i] = lax.ppermute(send, both, ring_pairs)]
    unnamed x74 -> x66, local copies, waits for them, and re-layouts: 37.6 us -> 36.8 us
  transfers between devices with their start and end apart: 35 -> 36, of which waited for: 21 -> 20; matrix products, arithmetic and copies ran while one was open for 36% -> 37% of each run, Pallas kernels for 0% -> 0%
where the time goes in v2:
time: 323 us; the launch traced here: 318 us
  waiting for transfers between devices  108 us (33%)
  matrix products  54.3 us (17%)
  local copies, waits for them, and re-layouts  45.2 us (14%)
  starting transfers between devices  44.3 us (14%)
  between operations  35.2 us (11%)
  other arithmetic  29.2 us (9%)
    ppermute x14, waiting for transfers between devices, on_device(): acc[i] = lax.ppermute(send, both, ring_pairs)  79.7 us
    unnamed x66, local copies, waits for them, and re-layouts  36.8 us
    ppermute x14, waiting for transfers between devices, on_device(): moving[i] = lax.ppermute(moving[i], both, ring_pairs)  25.1 us
    ppermute x14, starting transfers between devices, on_device(): moving[i] = lax.ppermute(moving[i], both, ring_pairs)  23.5 us
    dot_general x2, matrix products, on_device(): jnp.dot(normed, query_full, preferred_element_type=jnp.float32)  19.3 us
    mul x2, other arithmetic, fast_prune(): weight.reshape(keep.shape[0], step_r, cols) * mask[:, None, :]  18.9 us
    ppermute x14, starting transfers between devices, on_device(): acc[i] = lax.ppermute(send, both, ring_pairs)  14.4 us
    dot_general x16, matrix products, chunk(): return jnp.dot(context, cols, preferred_element_type=jnp.float32)  13.1 us
  transfers between devices with their start and end apart: 36, of which 20 were waited for; matrix products, arithmetic and copies ran while one was open for 37% of the time, Pallas kernels for 0%

profile of v2, /device:TPU:0, one launch (start us, length us, event | category | flops | bytes accessed | tf_op | source)
XLA Modules:
  0.0 318.5 jit_solution(2506566234318799472)
XLA Ops:
  9.1 3.1 collective-permute-start.9
  13.1 1.6 collective-permute-start
  15.5 4.6 %collective-permute-done.9 = bf16[296,1024]{1,0:T(8,128)(2,1)} collective-permute-done((bf16[296,1024]{1,0:T(8,128)(2,1)S(1)}, bf16[296,1024]{1,0:T(8,128)(2,1)}, u32[]{:S(2)}, u32[]{:S(2)}) %collective-permute-start.9) | collective-permute-done | bytes 606240 | tf_op jit(solution)/shard_map/ppermute | solution.py:127
  20.2 2.1 collective-permute-start.10
  36.2 1.6 collective-permute-start.1
  39.1 1.6 collective-permute-start.11
  41.4 5.0 %collective-permute-done.1 = bf16[304,1024]{1,0:T(8,128)(2,1)S(1)} collective-permute-done((bf16[304,1024]{1,0:T(8,128)(2,1)S(1)}, bf16[304,1024]{1,0:T(8,128)(2,1)S(1)}, u32[]{:S(2)}, u32[]{:S(2)}) %collective-permute-start.1) | collective-permute-done | bytes 622624 | tf_op jit(solution)/shard_map/ppermute | solution.py:127
  46.4 1.6 collective-permute-start.2
  49.1 4.0 %collective-permute-done.11 = bf16[296,1024]{1,0:T(8,128)(2,1)} collective-permute-done((bf16[296,1024]{1,0:T(8,128)(2,1)S(1)}, bf16[296,1024]{1,0:T(8,128)(2,1)}, u32[]{:S(2)}, u32[]{:S(2)}) %collective-permute-start.11) | collective-permute-done | bytes 606240 | tf_op jit(solution)/shard_map/ppermute | solution.py:127
  53.0 1.6 collective-permute-start.12
  54.6 5.0 %collective-permute-done.2 = bf16[304,1024]{1,0:T(8,128)(2,1)S(1)} collective-permute-done((bf16[304,1024]{1,0:T(8,128)(2,1)S(1)}, bf16[304,1024]{1,0:T(8,128)(2,1)S(1)}, u32[]{:S(2)}, u32[]{:S(2)}) %collective-permute-start.2) | collective-permute-done | bytes 622624 | tf_op jit(solution)/shard_map/ppermute | solution.py:127
  59.6 1.6 collective-permute-start.3
  64.4 1.1 multiply_cosine_fusion
  68.7 1.8 all-gather
  71.7 1.6 collective-permute-start.13
  73.4 2.0 constant_dynamic-update-slice_fusion.15
  75.4 1.5 collective-permute-start.4
  77.8 2.0 constant_dynamic-update-slice_fusion.14
  80.6 2.0 constant_dynamic-update-slice_fusion.13
  84.6 4.1 %collective-permute-done.4 = bf16[304,1024]{1,0:T(8,128)(2,1)S(1)} collective-permute-done((bf16[304,1024]{1,0:T(8,128)(2,1)}, bf16[304,1024]{1,0:T(8,128)(2,1)S(1)}, u32[]{:S(2)}, u32[]{:S(2)}) %collective-permute-start.4) | collective-permute-done | bytes 622624 | tf_op jit(solution)/shard_map/ppermute | solution.py:127
  88.7 1.6 collective-permute-start.5
  90.3 2.0 constant_dynamic-update-slice_fusion.12
  92.3 2.0 constant_dynamic-update-slice_fusion.3
  96.2 1.5 collective-permute-start.15
  97.7 2.0 constant_dynamic-update-slice_fusion.10
  99.6 2.3 collective-permute-done.5
  101.9 1.6 collective-permute-start.6
  104.4 1.2 dynamic-slice_dynamic-update-slice_fusion.15
  105.6 1.4 dynamic-slice_dynamic-update-slice_fusion.14
  114.7 2.6 fusion.61
  119.9 2.4 fusion.64
  122.4 3.8 %collective-permute-start.7 = (bf16[304,128]{0,1:T(8,128)(2,1)S(1)}, bf16[304,128]{0,1:T(8,128)(2,1)S(1)}, u32[]{:S(2)}, u32[]{:S(2)}) collective-permute-start(bf16[304,128]{0,1:T(8,128)(2,1)S(1)} %get-tuple-element.53), channel_id=1, source_target_pairs={{0,2},{2,6},{4,10},{6,14},{8,0},{10,4},{12,8},{14,12},{1,3},{3,7},... | collective-permute-start | bytes 233480 | tf_op jit(solution)/shard_map/ppermute | solution.py:160
  126.9 2.2 collective-permute-done.7
  130.0 10.9 %fusion = bf16[8192,1024]{1,0:T(8,128)(2,1)S(1)} fusion(bf16[4096,1024]{1,0:T(8,128)(2,1)} %collective-permute-done.18, bf16[4096,1024]{1,0:T(8,128)(2,1)S(1)} %bitcast.129, pred[]{:T(512)S(6)} %eq.65, bf16[128,1024]{1,0:T(8,128)(2,1)S(1)} %copy.35), kind=kLoop, calls=%fused_computation.1 | loop fusion | flops 109051904 | bytes 33816576 | tf_op jit(solution)/shard_map/mul | solution.py:71
  140.9 1.5 dynamic-slice_dynamic-update-slice_fusion.7
  142.4 1.5 dynamic-slice_dynamic-update-slice_fusion.6
  143.9 1.5 dynamic-slice_dynamic-update-slice_fusion.5
  145.4 1.6 dynamic-slice_dynamic-update-slice_fusion.4
  147.0 1.5 dynamic-slice_dynamic-update-slice_fusion.3
  148.5 1.6 dynamic-slice_dynamic-update-slice_fusion.2
  150.0 1.5 dynamic-slice_dynamic-update-slice_fusion.1
  151.5 1.5 dynamic-slice_dynamic-update-slice_fusion
  153.0 10.3 %fusion.47 = f32[296,1024]{1,0:T(8,128)S(1)} fusion(bf16[8192,1024]{1,0:T(8,128)(2,1)} %dynamic-slice_dynamic-update-slice_fusion, bf16[296,8192]{1,0:T(8,128)(2,1)} %copy-done.1, f32[8192]{0:T(1024)S(1)} %constant_dynamic-update-slice_fusion.17, f32[296]{0:T(512)S(1)} %add_rsqrt_fusion), kind=kOutput, calls=%fused_computation.67 | convolution fusion | flops 4975755264 | bytes 22873248 | tf_op jit(solution)/shard_map/dot_general | solution.py:153
  163.3 9.0 %fusion.43 = f32[304,1024]{1,0:T(8,128)S(1)} fusion(bf16[8192,1024]{1,0:T(8,128)(2,1)} %dynamic-slice_dynamic-update-slice_fusion, bf16[304,8192]{1,0:T(8,128)(2,1)S(1)} %constant_dynamic-update-slice_fusion, f32[8192]{0:T(1024)S(1)} %constant_dynamic-update-slice_fusion.17, f32[304]{0:T(512)S(1)} %add_rsqrt_fusion.1), kind=kOutput, calls=%fused_computation.65 | convolution fusion | flops 5110235136 | bytes 23037120 | tf_op jit(solution)/shard_map/dot_general | solution.py:153
  175.2 2.1 fusion.7
  177.2 10.7 %fusion.59 = bf16[8,38,8,128]{3,2,1,0:T(8,128)(2,1)S(1)} fusion(f32[600,304,8]{0,1,2:T(8,128)S(1)} %get-tuple-element.77, f32[8,304]{1,0:T(8,128)S(1)} %get-tuple-element.76, pred[304,600]{1,0:T(8,128)(4,1)S(1)} %slice.60, bf16[296,128]{0,1:T(8,128)(2,1)S(1)} %get-tuple-element.51, bf16[304,128]{0,1:T(8,128)(2,1)S(1)} %get-tuple-element.49), kind=kOutput, calls=%fused_computation.73 | convolution fusion | flops 380010496 | bytes 6805120 | tf_op jit(solution)/shard_map/hqk,kd->qhd/dot_general | solution.py:182
  187.9 8.0 %bitcast_multiply_fusion = bf16[1024,8192]{1,0:T(8,128)(2,1)S(1)} fusion(bf16[1024,8192]{1,0:T(8,128)(2,1)} %all-gather.6.cloned.1.call-done, bf16[16,8192]{1,0:T(8,128)(2,1)S(1)} %mul.390), kind=kLoop, calls=%fused_computation.2 | loop fusion | flops 8388608 | bytes 33816576 | tf_op jit(solution)/shard_map/mul | solution.py:71
  197.7 6.0 %collective-permute-start.20 = (bf16[304,1024]{1,0:T(8,128)(2,1)S(1)}, bf16[304,1024]{1,0:T(8,128)(2,1)S(1)}, u32[]{:S(2)}, u32[]{:S(2)}) collective-permute-start(bf16[304,1024]{1,0:T(8,128)(2,1)S(1)} %fusion.51), channel_id=1, source_target_pairs={{0,4},{4,8},{8,12},{12,14},{14,10},{10,6},{6,2},{2,0},{1,3},{5,1},... | collective-permute-start | bytes 1867784 | tf_op jit(solution)/shard_map/ppermute | solution.py:206
  203.7 1.9 fusion.8
  205.6 2.2 fusion.60
  219.7 7.6 %collective-permute-done.27 = bf16[296,1024]{1,0:T(8,128)(2,1)S(1)} collective-permute-done((bf16[296,1024]{1,0:T(8,128)(2,1)S(1)}, bf16[296,1024]{1,0:T(8,128)(2,1)S(1)}, u32[]{:S(2)}, u32[]{:S(2)}) %collective-permute-start.27) | collective-permute-done | bytes 606240 | tf_op jit(solution)/shard_map/ppermute | solution.py:206
  228.2 2.5 collective-permute-start.21
  230.7 6.9 %collective-permute-done.28 = bf16[296,1024]{1,0:T(8,128)(2,1)S(1)} collective-permute-done((bf16[296,1024]{1,0:T(8,128)(2,1)S(1)}, bf16[296,1024]{1,0:T(8,128)(2,1)S(1)}, u32[]{:S(2)}, u32[]{:S(2)}) %collective-permute-start.28) | collective-permute-done | bytes 606240 | tf_op jit(solution)/shard_map/ppermute | solution.py:206
  238.3 6.0 %collective-permute-done.21 = bf16[304,1024]{1,0:T(8,128)(2,1)S(1)} collective-permute-done((bf16[304,1024]{1,0:T(8,128)(2,1)S(1)}, bf16[304,1024]{1,0:T(8,128)(2,1)S(1)}, u32[]{:S(2)}, u32[]{:S(2)}) %collective-permute-start.21) | collective-permute-done | bytes 622624 | tf_op jit(solution)/shard_map/ppermute | solution.py:206
  245.0 5.8 %collective-permute-done.29 = bf16[296,1024]{1,0:T(8,128)(2,1)S(1)} collective-permute-done((bf16[296,1024]{1,0:T(8,128)(2,1)S(1)}, bf16[296,1024]{1,0:T(8,128)(2,1)S(1)}, u32[]{:S(2)}, u32[]{:S(2)}) %collective-permute-start.29) | collective-permute-done | bytes 606240 | tf_op jit(solution)/shard_map/ppermute | solution.py:206
  251.4 6.0 %collective-permute-done.22 = bf16[304,1024]{1,0:T(8,128)(2,1)S(1)} collective-permute-done((bf16[304,1024]{1,0:T(8,128)(2,1)S(1)}, bf16[304,1024]{1,0:T(8,128)(2,1)S(1)}, u32[]{:S(2)}, u32[]{:S(2)}) %collective-permute-start.22) | collective-permute-done | bytes 622624 | tf_op jit(solution)/shard_map/ppermute | solution.py:206
  258.1 5.8 %collective-permute-done.30 = bf16[296,1024]{1,0:T(8,128)(2,1)S(1)} collective-permute-done((bf16[296,1024]{1,0:T(8,128)(2,1)S(1)}, bf16[296,1024]{1,0:T(8,128)(2,1)S(1)}, u32[]{:S(2)}, u32[]{:S(2)}) %collective-permute-start.30) | collective-permute-done | bytes 606240 | tf_op jit(solution)/shard_map/ppermute | solution.py:206
  264.6 6.0 %collective-permute-done.23 = bf16[304,1024]{1,0:T(8,128)(2,1)S(1)} collective-permute-done((bf16[304,1024]{1,0:T(8,128)(2,1)S(1)}, bf16[304,1024]{1,0:T(8,128)(2,1)S(1)}, u32[]{:S(2)}, u32[]{:S(2)}) %collective-permute-start.23) | collective-permute-done | bytes 622624 | tf_op jit(solution)/shard_map/ppermute | solution.py:206
  271.3 5.8 %collective-permute-done.31 = bf16[296,1024]{1,0:T(8,128)(2,1)S(1)} collective-permute-done((bf16[296,1024]{1,0:T(8,128)(2,1)S(1)}, bf16[296,1024]{1,0:T(8,128)(2,1)S(1)}, u32[]{:S(2)}, u32[]{:S(2)}) %collective-permute-start.31) | collective-permute-done | bytes 606240 | tf_op jit(solution)/shard_map/ppermute | solution.py:206
  277.8 6.0 %collective-permute-done.24 = bf16[304,1024]{1,0:T(8,128)(2,1)S(1)} collective-permute-done((bf16[304,1024]{1,0:T(8,128)(2,1)S(1)}, bf16[304,1024]{1,0:T(8,128)(2,1)S(1)}, u32[]{:S(2)}, u32[]{:S(2)}) %collective-permute-start.24) | collective-permute-done | bytes 622624 | tf_op jit(solution)/shard_map/ppermute | solution.py:206
  284.5 5.8 %collective-permute-done.32 = bf16[296,1024]{1,0:T(8,128)(2,1)S(1)} collective-permute-done((bf16[296,1024]{1,0:T(8,128)(2,1)S(1)}, bf16[296,1024]{1,0:T(8,128)(2,1)S(1)}, u32[]{:S(2)}, u32[]{:S(2)}) %collective-permute-start.32) | collective-permute-done | bytes 606240 | tf_op jit(solution)/shard_map/ppermute | solution.py:206
  291.0 6.0 %collective-permute-done.25 = bf16[304,1024]{1,0:T(8,128)(2,1)S(1)} collective-permute-done((bf16[304,1024]{1,0:T(8,128)(2,1)S(1)}, bf16[304,1024]{1,0:T(8,128)(2,1)S(1)}, u32[]{:S(2)}, u32[]{:S(2)}) %collective-permute-start.25) | collective-permute-done | bytes 622624 | tf_op jit(solution)/shard_map/ppermute | solution.py:206
  297.6 5.8 %collective-permute-done.33 = bf16[296,1024]{1,0:T(8,128)(2,1)S(1)} collective-permute-done((bf16[296,1024]{1,0:T(8,128)(2,1)S(1)}, bf16[296,1024]{1,0:T(8,128)(2,1)S(1)}, u32[]{:S(2)}, u32[]{:S(2)}) %collective-permute-start.33) | collective-permute-done | bytes 606240 | tf_op jit(solution)/shard_map/ppermute | solution.py:206
  303.6 6.5 %collective-permute-done.26 = bf16[304,1024]{1,0:T(8,128)(2,1)S(1)} collective-permute-done((bf16[304,1024]{1,0:T(8,128)(2,1)S(1)}, bf16[304,1024]{1,0:T(8,128)(2,1)S(1)}, u32[]{:S(2)}, u32[]{:S(2)}) %collective-permute-start.26) | collective-permute-done | bytes 622624 | tf_op jit(solution)/shard_map/ppermute | solution.py:206
  (162 shorter events, 51.7 us)
Async XLA Ops:
  6.5 1.5 copy-start.2
  6.5 97.8 %all-gather.4.cloned.1.call-start = ((), (), s32[]{:S(2)}) async-start(), calls=%async_computation | async-start | bytes 6291456 | tf_op jit(solution)/shard_map/all_gather | solution.py:114
  7.3 7.4 %copy-start.8 = (s32[64,16]{0,1:T(8,128)S(1)}, s32[64,16]{0,1:T(8,128)}, u32[]{:S(2)}) copy-start(s32[64,16]{0,1:T(8,128)} %param.14) | copy-start | bytes 12292
  7.3 7.9 %copy-start.9 = (s32[1,4]{1,0:T(1,128)S(1)}, s32[1,4]{1,0:T(1,128)}, u32[]{:S(2)}) copy-start(s32[1,4]{1,0:T(1,128)} %param.18) | copy-start | bytes 52
  7.3 8.1 %copy-start.10 = (s32[1,4]{1,0:T(1,128)S(1)}, s32[1,4]{1,0:T(1,128)}, u32[]{:S(2)}) copy-start(s32[1,4]{1,0:T(1,128)} %param.19) | copy-start | bytes 52
  7.3 15.0 %copy-start.6 = (f32[8192]{0:T(1024)S(1)}, f32[8192]{0:T(1024)}, u32[]{:S(2)}) copy-start(f32[8192]{0:T(1024)} %param.12) | copy-start | bytes 98308
  7.3 15.0 %copy-start.11 = (s32[8]{0:T(128)S(1)}, s32[8]{0:T(128)}, u32[]{:S(2)}) copy-start(s32[8]{0:T(128)} %constant.166.clone) | copy-start | bytes 100
  7.3 26.8 %copy-start.5 = (s32[8]{0:T(128)S(1)}, s32[8]{0:T(128)}, u32[]{:S(2)}) copy-start(s32[8]{0:T(128)} %constant.167.clone) | copy-start | bytes 100
  7.3 180.6 %all-gather.6.cloned.1.call-start = ((), (), s32[]{:S(2)}) async-start(), calls=%async_computation.1 | async-start | bytes 25165824 | tf_op jit(solution)/shard_map/all_gather | solution.py:116
  8.1 60.6 %copy-start.7 = (s32[16,64]{1,0:T(8,128)S(1)}, s32[16,64]{1,0:T(8,128)}, u32[]{:S(2)}) copy-start(s32[16,64]{1,0:T(8,128)} %param.17) | copy-start | bytes 12292
  9.1 11.1 %collective-permute-start.9 = (bf16[296,1024]{1,0:T(8,128)(2,1)S(1)}, bf16[296,1024]{1,0:T(8,128)(2,1)}, u32[]{:S(2)}, u32[]{:S(2)}) collective-permute-start(bf16[296,1024]{1,0:T(8,128)(2,1)S(1)} %get-tuple-element.45), channel_id=1, source_target_pairs={{0,4},{4,8},{8,12},{12,14},{14,10},{10,6},{6,2},{2,0},{1,3},{5,1},... | collective-permute-start | bytes 1818632 | tf_op jit(solution)/shard_map/ppermute | solution.py:127
  13.1 23.1 %collective-permute-start = (bf16[304,1024]{1,0:T(8,128)(2,1)S(1)}, bf16[304,1024]{1,0:T(8,128)(2,1)S(1)}, u32[]{:S(2)}, u32[]{:S(2)}) collective-permute-start(bf16[304,1024]{1,0:T(8,128)(2,1)S(1)} %get-tuple-element.43), channel_id=1, source_target_pairs={{0,4},{4,8},{8,12},{12,14},{14,10},{10,6},{6,2},{2,0},{1,3},{5,1},... | collective-permute-start | bytes 1867784 | tf_op jit(solution)/shard_map/ppermute | solution.py:127
  14.6 56.8 %collective-permute-start.19 = (s32[64,16]{0,1:T(8,128)S(1)}, s32[64,16]{0,1:T(8,128)S(1)}, u32[]{:S(2)}, u32[]{:S(2)}) collective-permute-start(s32[64,16]{0,1:T(8,128)S(1)} %copy-done.8), channel_id=1, source_target_pairs={{0,1},{1,0},{2,3},{3,2},{4,5},{5,4},{6,7},{7,6},{8,9},{9,8},{10,11... | collective-permute-start | bytes 12296 | tf_op jit(solution)/shard_map/ppermute | solution.py:106
  14.6 115.3 %collective-permute-start.18 = (bf16[4096,1024]{1,0:T(8,128)(2,1)}, bf16[4096,1024]{1,0:T(8,128)(2,1)}, u32[]{:S(2)}, u32[]{:S(2)}) collective-permute-start(bf16[4096,1024]{1,0:T(8,128)(2,1)} %param.13), channel_id=1, source_target_pairs={{0,1},{1,0},{2,3},{3,2},{4,5},{5,4},{6,7},{7,6},{8,9},{9,8},{10,11... | collective-permute-start | bytes 25165832 | tf_op jit(solution)/shard_map/ppermute | solution.py:106
  20.2 18.9 %collective-permute-start.10 = (bf16[296,1024]{1,0:T(8,128)(2,1)}, bf16[296,1024]{1,0:T(8,128)(2,1)S(1)}, u32[]{:S(2)}, u32[]{:S(2)}) collective-permute-start(bf16[296,1024]{1,0:T(8,128)(2,1)} %collective-permute-done.9), channel_id=1, source_target_pairs={{0,4},{4,8},{8,12},{12,14},{14,10},{10,6},{6,2},{2,0},{1,3},{5,1},... | collective-permute-start | bytes 1818632 | tf_op jit(solution)/shard_map/ppermute | solution.py:127
  36.2 10.3 %collective-permute-start.1 = (bf16[304,1024]{1,0:T(8,128)(2,1)S(1)}, bf16[304,1024]{1,0:T(8,128)(2,1)S(1)}, u32[]{:S(2)}, u32[]{:S(2)}) collective-permute-start(bf16[304,1024]{1,0:T(8,128)(2,1)S(1)} %collective-permute-done), channel_id=1, source_target_pairs={{0,4},{4,8},{8,12},{12,14},{14,10},{10,6},{6,2},{2,0},{1,3},{5,1},... | collective-permute-start | bytes 1867784 | tf_op jit(solution)/shard_map/ppermute | solution.py:127
  39.1 25.3 %copy-start.3 = (bf16[296,1024]{1,0:T(8,128)(2,1)}, bf16[296,1024]{1,0:T(8,128)(2,1)S(1)}, u32[]{:S(2)}) copy-start(bf16[296,1024]{1,0:T(8,128)(2,1)S(1)} %collective-permute-done.10) | copy-start | bytes 1818628
  39.1 14.0 %collective-permute-start.11 = (bf16[296,1024]{1,0:T(8,128)(2,1)S(1)}, bf16[296,1024]{1,0:T(8,128)(2,1)}, u32[]{:S(2)}, u32[]{:S(2)}) collective-permute-start(bf16[296,1024]{1,0:T(8,128)(2,1)S(1)} %collective-permute-done.10), channel_id=1, source_target_pairs={{0,4},{4,8},{8,12},{12,14},{14,10},{10,6},{6,2},{2,0},{1,3},{5,1},... | collective-permute-start | bytes 1818632 | tf_op jit(solution)/shard_map/ppermute | solution.py:127
  46.4 13.2 %collective-permute-start.2 = (bf16[304,1024]{1,0:T(8,128)(2,1)S(1)}, bf16[304,1024]{1,0:T(8,128)(2,1)S(1)}, u32[]{:S(2)}, u32[]{:S(2)}) collective-permute-start(bf16[304,1024]{1,0:T(8,128)(2,1)S(1)} %collective-permute-done.1), channel_id=1, source_target_pairs={{0,4},{4,8},{8,12},{12,14},{14,10},{10,6},{6,2},{2,0},{1,3},{5,1},... | collective-permute-start | bytes 1867784 | tf_op jit(solution)/shard_map/ppermute | solution.py:127
  53.0 18.7 %collective-permute-start.12 = (bf16[296,1024]{1,0:T(8,128)(2,1)}, bf16[296,1024]{1,0:T(8,128)(2,1)}, u32[]{:S(2)}, u32[]{:S(2)}) collective-permute-start(bf16[296,1024]{1,0:T(8,128)(2,1)} %collective-permute-done.11), channel_id=1, source_target_pairs={{0,4},{4,8},{8,12},{12,14},{14,10},{10,6},{6,2},{2,0},{1,3},{5,1},... | collective-permute-start | bytes 1818632 | tf_op jit(solution)/shard_map/ppermute | solution.py:127
  59.6 15.7 %collective-permute-start.3 = (bf16[304,1024]{1,0:T(8,128)(2,1)S(1)}, bf16[304,1024]{1,0:T(8,128)(2,1)}, u32[]{:S(2)}, u32[]{:S(2)}) collective-permute-start(bf16[304,1024]{1,0:T(8,128)(2,1)S(1)} %collective-permute-done.2), channel_id=1, source_target_pairs={{0,4},{4,8},{8,12},{12,14},{14,10},{10,6},{6,2},{2,0},{1,3},{5,1},... | collective-permute-start | bytes 1867784 | tf_op jit(solution)/shard_map/ppermute | solution.py:127
  71.7 10.9 %collective-permute-start.13 = (bf16[296,1024]{1,0:T(8,128)(2,1)}, bf16[296,1024]{1,0:T(8,128)(2,1)S(1)}, u32[]{:S(2)}, u32[]{:S(2)}) collective-permute-start(bf16[296,1024]{1,0:T(8,128)(2,1)} %collective-permute-done.12), channel_id=1, source_target_pairs={{0,4},{4,8},{8,12},{12,14},{14,10},{10,6},{6,2},{2,0},{1,3},{5,1},... | collective-permute-start | bytes 1818632 | tf_op jit(solution)/shard_map/ppermute | solution.py:127
  75.4 13.4 %collective-permute-start.4 = (bf16[304,1024]{1,0:T(8,128)(2,1)}, bf16[304,1024]{1,0:T(8,128)(2,1)S(1)}, u32[]{:S(2)}, u32[]{:S(2)}) collective-permute-start(bf16[304,1024]{1,0:T(8,128)(2,1)} %collective-permute-done.3), channel_id=1, source_target_pairs={{0,4},{4,8},{8,12},{12,14},{14,10},{10,6},{6,2},{2,0},{1,3},{5,1},... | collective-permute-start | bytes 1867784 | tf_op jit(solution)/shard_map/ppermute | solution.py:127
  82.6 13.5 %collective-permute-start.14 = (bf16[296,1024]{1,0:T(8,128)(2,1)S(1)}, bf16[296,1024]{1,0:T(8,128)(2,1)}, u32[]{:S(2)}, u32[]{:S(2)}) collective-permute-start(bf16[296,1024]{1,0:T(8,128)(2,1)S(1)} %collective-permute-done.13), channel_id=1, source_target_pairs={{0,4},{4,8},{8,12},{12,14},{14,10},{10,6},{6,2},{2,0},{1,3},{5,1},... | collective-permute-start | bytes 1818632 | tf_op jit(solution)/shard_map/ppermute | solution.py:127
  88.7 13.2 %collective-permute-start.5 = (bf16[304,1024]{1,0:T(8,128)(2,1)S(1)}, bf16[304,1024]{1,0:T(8,128)(2,1)S(1)}, u32[]{:S(2)}, u32[]{:S(2)}) collective-permute-start(bf16[304,1024]{1,0:T(8,128)(2,1)S(1)} %collective-permute-done.4), channel_id=1, source_target_pairs={{0,4},{4,8},{8,12},{12,14},{14,10},{10,6},{6,2},{2,0},{1,3},{5,1},... | collective-permute-start | bytes 1867784 | tf_op jit(solution)/shard_map/ppermute | solution.py:127
  96.2 17.4 %collective-permute-start.15 = (bf16[296,1024]{1,0:T(8,128)(2,1)}, bf16[296,1024]{1,0:T(8,128)(2,1)S(1)}, u32[]{:S(2)}, u32[]{:S(2)}) collective-permute-start(bf16[296,1024]{1,0:T(8,128)(2,1)} %collective-permute-done.14), channel_id=1, source_target_pairs={{0,4},{4,8},{8,12},{12,14},{14,10},{10,6},{6,2},{2,0},{1,3},{5,1},... | collective-permute-start | bytes 1818632 | tf_op jit(solution)/shard_map/ppermute | solution.py:127
  101.9 16.8 %collective-permute-start.6 = (bf16[304,1024]{1,0:T(8,128)(2,1)S(1)}, bf16[304,1024]{1,0:T(8,128)(2,1)S(1)}, u32[]{:S(2)}, u32[]{:S(2)}) collective-permute-start(bf16[304,1024]{1,0:T(8,128)(2,1)S(1)} %collective-permute-done.5), channel_id=1, source_target_pairs={{0,4},{4,8},{8,12},{12,14},{14,10},{10,6},{6,2},{2,0},{1,3},{5,1},... | collective-permute-start | bytes 1867784 | tf_op jit(solution)/shard_map/ppermute | solution.py:127
  104.4 9.2 %copy-start = (bf16[296,8192]{1,0:T(8,128)(2,1)S(1)}, bf16[296,8192]{1,0:T(8,128)(2,1)}, u32[]{:S(2)}) copy-start(bf16[296,8192]{1,0:T(8,128)(2,1)} %constant_dynamic-update-slice_fusion.10) | copy-start | bytes 14548996
  113.6 3.6 %copy-start.1 = (bf16[296,8192]{1,0:T(8,128)(2,1)}, bf16[296,8192]{1,0:T(8,128)(2,1)S(1)}, u32[]{:S(2)}) copy-start(bf16[296,8192]{1,0:T(8,128)(2,1)S(1)} %constant_dynamic-update-slice_fusion.9) | copy-start | bytes 14548996
  113.6 5.1 %slice-start.2 = ((s8[4980736]{0:T(1024)(128)(4,1)}), s8[4194304]{0:T(1024)(128)(4,1)S(1)}, s32[]{:S(2)}) async-start(s8[4980736]{0:T(1024)(128)(4,1)} %bitcast.130), calls=%async_computation.4 | async-start | bytes 8388608
  114.7 4.1 %slice-start.3 = ((s8[4980736]{0:T(1024)(128)(4,1)}), s8[786432]{0:T(1024)(128)(4,1)S(1)}, s32[]{:S(2)}) async-start(s8[4980736]{0:T(1024)(128)(4,1)} %bitcast.130), calls=%async_computation.5 | async-start | bytes 1572864
  117.3 9.6 %collective-permute-start.16 = (bf16[296,128]{0,1:T(8,128)(2,1)S(1)}, bf16[296,128]{0,1:T(8,128)(2,1)S(1)}, u32[]{:S(2)}, u32[]{:S(2)}) collective-permute-start(bf16[296,128]{0,1:T(8,128)(2,1)S(1)} %get-tuple-element.55), channel_id=1, source_target_pairs={{0,2},{2,6},{4,10},{6,14},{8,0},{10,4},{12,8},{14,12},{1,3},{3,7},... | collective-permute-start | bytes 227336 | tf_op jit(solution)/shard_map/ppermute | solution.py:160
  117.8 9.1 %collective-permute-start.17 = (bf16[296,128]{0,1:T(8,128)(2,1)S(1)}, bf16[296,128]{0,1:T(8,128)(2,1)S(1)}, u32[]{:S(2)}, u32[]{:S(2)}) collective-permute-start(bf16[296,128]{0,1:T(8,128)(2,1)S(1)} %get-tuple-element.56), channel_id=1, source_target_pairs={{0,0},{2,4},{4,8},{6,12},{8,2},{10,6},{12,10},{14,14},{1,1},{3,5},... | collective-permute-start | bytes 227336 | tf_op jit(solution)/shard_map/ppermute | solution.py:159
  119.9 10.0 %slice-start = ((s8[8388608]{0:T(1024)(128)(4,1)}), s8[4194304]{0:T(1024)(128)(4,1)S(1)}, s32[]{:S(2)}) async-start(s8[8388608]{0:T(1024)(128)(4,1)} %bitcast.128), calls=%async_computation.2 | async-start | bytes 8388608
  119.9 10.0 %slice-start.1 = ((s8[8388608]{0:T(1024)(128)(4,1)}), s8[4194304]{0:T(1024)(128)(4,1)S(1)}, s32[]{:S(2)}) async-start(s8[8388608]{0:T(1024)(128)(4,1)} %bitcast.128), calls=%async_computation.3 | async-start | bytes 8388608
  122.4 6.7 %collective-permute-start.7 = (bf16[304,128]{0,1:T(8,128)(2,1)S(1)}, bf16[304,128]{0,1:T(8,128)(2,1)S(1)}, u32[]{:S(2)}, u32[]{:S(2)}) collective-permute-start(bf16[304,128]{0,1:T(8,128)(2,1)S(1)} %get-tuple-element.53), channel_id=1, source_target_pairs={{0,2},{2,6},{4,10},{6,14},{8,0},{10,4},{12,8},{14,12},{1,3},{3,7},... | collective-permute-start | bytes 233480 | tf_op jit(solution)/shard_map/ppermute | solution.py:160
  126.2 2.9 collective-permute-start.8
  195.9 7.7 %copy-start.4 = (pred[296,600]{1,0:T(8,128)(4,1)S(1)}, pred[296,600]{1,0:T(8,128)(4,1)}, u32[]{:S(2)}) copy-start(pred[296,600]{1,0:T(8,128)(4,1)} %slice.67) | copy-start | bytes 532804
  197.7 30.3 %collective-permute-start.20 = (bf16[304,1024]{1,0:T(8,128)(2,1)S(1)}, bf16[304,1024]{1,0:T(8,128)(2,1)S(1)}, u32[]{:S(2)}, u32[]{:S(2)}) collective-permute-start(bf16[304,1024]{1,0:T(8,128)(2,1)S(1)} %fusion.51), channel_id=1, source_target_pairs={{0,4},{4,8},{8,12},{12,14},{14,10},{10,6},{6,2},{2,0},{1,3},{5,1},... | collective-permute-start | bytes 1867784 | tf_op jit(solution)/shard_map/ppermute | solution.py:206
  217.0 10.3 %collective-permute-start.27 = (bf16[296,1024]{1,0:T(8,128)(2,1)S(1)}, bf16[296,1024]{1,0:T(8,128)(2,1)S(1)}, u32[]{:S(2)}, u32[]{:S(2)}) collective-permute-start(bf16[296,1024]{1,0:T(8,128)(2,1)S(1)} %fusion.55), channel_id=1, source_target_pairs={{0,4},{4,8},{8,12},{12,14},{14,10},{10,6},{6,2},{2,0},{1,3},{5,1},... | collective-permute-start | bytes 1818632 | tf_op jit(solution)/shard_map/ppermute | solution.py:206
  227.5 10.1 %collective-permute-start.28 = (bf16[296,1024]{1,0:T(8,128)(2,1)S(1)}, bf16[296,1024]{1,0:T(8,128)(2,1)S(1)}, u32[]{:S(2)}, u32[]{:S(2)}) collective-permute-start(bf16[296,1024]{1,0:T(8,128)(2,1)S(1)} %add_convert_fusion.14), channel_id=1, source_target_pairs={{0,4},{4,8},{8,12},{12,14},{14,10},{10,6},{6,2},{2,0},{1,3},{5,1},... | collective-permute-start | bytes 1818632 | tf_op jit(solution)/shard_map/ppermute | solution.py:206
  228.2 16.1 %collective-permute-start.21 = (bf16[304,1024]{1,0:T(8,128)(2,1)S(1)}, bf16[304,1024]{1,0:T(8,128)(2,1)S(1)}, u32[]{:S(2)}, u32[]{:S(2)}) collective-permute-start(bf16[304,1024]{1,0:T(8,128)(2,1)S(1)} %add_convert_fusion.7), channel_id=1, source_target_pairs={{0,4},{4,8},{8,12},{12,14},{14,10},{10,6},{6,2},{2,0},{1,3},{5,1},... | collective-permute-start | bytes 1867784 | tf_op jit(solution)/shard_map/ppermute | solution.py:206
  237.8 13.0 %collective-permute-start.29 = (bf16[296,1024]{1,0:T(8,128)(2,1)S(1)}, bf16[296,1024]{1,0:T(8,128)(2,1)S(1)}, u32[]{:S(2)}, u32[]{:S(2)}) collective-permute-start(bf16[296,1024]{1,0:T(8,128)(2,1)S(1)} %add_convert_fusion.13), channel_id=1, source_target_pairs={{0,4},{4,8},{8,12},{12,14},{14,10},{10,6},{6,2},{2,0},{1,3},{5,1},... | collective-permute-start | bytes 1818632 | tf_op jit(solution)/shard_map/ppermute | solution.py:206
  244.5 13.0 %collective-permute-start.22 = (bf16[304,1024]{1,0:T(8,128)(2,1)S(1)}, bf16[304,1024]{1,0:T(8,128)(2,1)S(1)}, u32[]{:S(2)}, u32[]{:S(2)}) collective-permute-start(bf16[304,1024]{1,0:T(8,128)(2,1)S(1)} %add_convert_fusion.6), channel_id=1, source_target_pairs={{0,4},{4,8},{8,12},{12,14},{14,10},{10,6},{6,2},{2,0},{1,3},{5,1},... | collective-permute-start | bytes 1867784 | tf_op jit(solution)/shard_map/ppermute | solution.py:206
  250.9 13.0 %collective-permute-start.30 = (bf16[296,1024]{1,0:T(8,128)(2,1)S(1)}, bf16[296,1024]{1,0:T(8,128)(2,1)S(1)}, u32[]{:S(2)}, u32[]{:S(2)}) collective-permute-start(bf16[296,1024]{1,0:T(8,128)(2,1)S(1)} %add_convert_fusion.12), channel_id=1, source_target_pairs={{0,4},{4,8},{8,12},{12,14},{14,10},{10,6},{6,2},{2,0},{1,3},{5,1},... | collective-permute-start | bytes 1818632 | tf_op jit(solution)/shard_map/ppermute | solution.py:206
  257.6 12.9 %collective-permute-start.23 = (bf16[304,1024]{1,0:T(8,128)(2,1)S(1)}, bf16[304,1024]{1,0:T(8,128)(2,1)S(1)}, u32[]{:S(2)}, u32[]{:S(2)}) collective-permute-start(bf16[304,1024]{1,0:T(8,128)(2,1)S(1)} %add_convert_fusion.5), channel_id=1, source_target_pairs={{0,4},{4,8},{8,12},{12,14},{14,10},{10,6},{6,2},{2,0},{1,3},{5,1},... | collective-permute-start | bytes 1867784 | tf_op jit(solution)/shard_map/ppermute | solution.py:206
  264.1 13.0 %collective-permute-start.31 = (bf16[296,1024]{1,0:T(8,128)(2,1)S(1)}, bf16[296,1024]{1,0:T(8,128)(2,1)S(1)}, u32[]{:S(2)}, u32[]{:S(2)}) collective-permute-start(bf16[296,1024]{1,0:T(8,128)(2,1)S(1)} %add_convert_fusion.11), channel_id=1, source_target_pairs={{0,4},{4,8},{8,12},{12,14},{14,10},{10,6},{6,2},{2,0},{1,3},{5,1},... | collective-permute-start | bytes 1818632 | tf_op jit(solution)/shard_map/ppermute | solution.py:206
  270.8 12.9 %collective-permute-start.24 = (bf16[304,1024]{1,0:T(8,128)(2,1)S(1)}, bf16[304,1024]{1,0:T(8,128)(2,1)S(1)}, u32[]{:S(2)}, u32[]{:S(2)}) collective-permute-start(bf16[304,1024]{1,0:T(8,128)(2,1)S(1)} %add_convert_fusion.4), channel_id=1, source_target_pairs={{0,4},{4,8},{8,12},{12,14},{14,10},{10,6},{6,2},{2,0},{1,3},{5,1},... | collective-permute-start | bytes 1867784 | tf_op jit(solution)/shard_map/ppermute | solution.py:206
  277.3 13.0 %collective-permute-start.32 = (bf16[296,1024]{1,0:T(8,128)(2,1)S(1)}, bf16[296,1024]{1,0:T(8,128)(2,1)S(1)}, u32[]{:S(2)}, u32[]{:S(2)}) collective-permute-start(bf16[296,1024]{1,0:T(8,128)(2,1)S(1)} %add_convert_fusion.10), channel_id=1, source_target_pairs={{0,4},{4,8},{8,12},{12,14},{14,10},{10,6},{6,2},{2,0},{1,3},{5,1},... | collective-permute-start | bytes 1818632 | tf_op jit(solution)/shard_map/ppermute | solution.py:206
  284.0 12.9 %collective-permute-start.25 = (bf16[304,1024]{1,0:T(8,128)(2,1)S(1)}, bf16[304,1024]{1,0:T(8,128)(2,1)S(1)}, u32[]{:S(2)}, u32[]{:S(2)}) collective-permute-start(bf16[304,1024]{1,0:T(8,128)(2,1)S(1)} %add_convert_fusion.3), channel_id=1, source_target_pairs={{0,4},{4,8},{8,12},{12,14},{14,10},{10,6},{6,2},{2,0},{1,3},{5,1},... | collective-permute-start | bytes 1867784 | tf_op jit(solution)/shard_map/ppermute | solution.py:206
  290.5 13.0 %collective-permute-start.33 = (bf16[296,1024]{1,0:T(8,128)(2,1)S(1)}, bf16[296,1024]{1,0:T(8,128)(2,1)S(1)}, u32[]{:S(2)}, u32[]{:S(2)}) collective-permute-start(bf16[296,1024]{1,0:T(8,128)(2,1)S(1)} %add_convert_fusion.9), channel_id=1, source_target_pairs={{0,4},{4,8},{8,12},{12,14},{14,10},{10,6},{6,2},{2,0},{1,3},{5,1},... | collective-permute-start | bytes 1818632 | tf_op jit(solution)/shard_map/ppermute | solution.py:206
  297.1 12.9 %collective-permute-start.26 = (bf16[304,1024]{1,0:T(8,128)(2,1)S(1)}, bf16[304,1024]{1,0:T(8,128)(2,1)S(1)}, u32[]{:S(2)}, u32[]{:S(2)}) collective-permute-start(bf16[304,1024]{1,0:T(8,128)(2,1)S(1)} %add_convert_fusion.2), channel_id=1, source_target_pairs={{0,4},{4,8},{8,12},{12,14},{14,10},{10,6},{6,2},{2,0},{1,3},{5,1},... | collective-permute-start | bytes 1867784 | tf_op jit(solution)/shard_map/ppermute | solution.py:206
Sparse Core Ops, SparseCore 0:
  8.9 19.0 all-gather.3
  29.5 31.2 all-gather.5
